TPU v7x, 256 devices: a whole 4x4x8 slice. The times are simulated.
256 devices in a mesh: row: 16 (over z_hi, x, core), col: 16 (over y, z_lo).
Axes of the slice: x: 4, y: 4, z: 8 (z_hi: 2, z_lo: 4; z = z_hi * 4 + z_lo), core: 2. Of those that a mesh axis runs over, the one named last changes fastest.
Arguments:
- points: float32 [64, 32768], P(None, ('row', 'col')), may hold values from -24 to 24, as said below
- embedding: float32 [2, 32768], P(None, ('row', 'col')), may hold values from -8 to 8
- precision: float32 [32768], P(('row', 'col')), may hold values from 0.05 to 2
Outputs:
- force: float32 [2, 32768], P(None, ('row', 'col'))
- calibrated: float32 [32768], P(('row', 'col'))
Inputs may be any that keep to these rules, and one draw needn't show every extreme that they name: `points`: each point's coordinates are normal values times a positive scale of that point.
All inputs are finite; a program needn't handle non-finite values.
Results may differ from a plain program's by a relative error of at most 0.0003.
Values sent between devices are 32-bit elements; how exact they have to be, the bound alone decides.
No kernel may reach another device: no remote copies, remote signals or barrier semaphores. Data moves between devices by JAX's collectives and lax.ppermute only.
A program may use at most 64 MiB of HBM per device.

v0:
```python
import math

import jax
import jax.numpy as jnp
from jax import lax
from jax.sharding import PartitionSpec as P

PERP = 30


def newton_update(zsum, first, second, start_prec):
    entropy = jnp.log(zsum) + start_prec * first / zsum
    spread = second / zsum - (first / zsum) ** 2
    factor = jnp.clip(
        (entropy - math.log(PERP)) / jnp.maximum(start_prec * start_prec * spread, 1.0), -2.0, 2.0
    )
    return start_prec * jnp.exp(factor)


def body(points, embedding, precision):
    per_dev = points.shape[1]
    width = points.shape[0]
    col_count = lax.axis_size("col")
    row_count = lax.axis_size("row")
    packed = jnp.concatenate([points, embedding, precision[None, :]], axis=0)
    row_pack = lax.all_gather(packed, "col", axis=1, tiled=True)
    col_pack = lax.all_gather(packed, "row", axis=1, tiled=True)
    rows_total = per_dev * col_count
    cols_total = per_dev * row_count
    total = rows_total * row_count
    row_coords = row_pack[:width]
    col_coords = col_pack[:width]
    row_map = row_pack[width : width + 2]
    col_map = col_pack[width : width + 2]
    row_prec = row_pack[width + 2]
    row_sq = jnp.sum(row_coords * row_coords, axis=0)
    col_sq = jnp.sum(col_coords * col_coords, axis=0)
    row_ids = lax.axis_index("row") * rows_total + jnp.arange(rows_total, dtype=jnp.int32)
    col_pos = jnp.arange(cols_total, dtype=jnp.int32)
    col_ids = col_pos // per_dev * rows_total + lax.axis_index("col") * per_dev + col_pos % per_dev
    block_rows = min(rows_total, 256)
    blocks = rows_total // block_rows
    own_start = lax.axis_index("col") * per_dev

    def slice_rows(values, start):
        return lax.dynamic_slice_in_dim(values, start, block_rows, values.ndim - 1)

    def distances(start):
        part = slice_rows(row_coords, start)
        inner = lax.dot_general(
            part,
            col_coords,
            (((0,), (0,)), ((), ())),
            precision=lax.Precision.HIGHEST,
            preferred_element_type=jnp.float32,
        )
        distance = jnp.maximum(
            slice_rows(row_sq, start)[:, None] + col_sq[None, :] - 2.0 * inner, 0.0
        )
        itself = slice_rows(row_ids, start)[:, None] == col_ids[None, :]
        return (distance, itself)

    def kernel_of(start, itself):
        part_y = slice_rows(row_map, start)
        delta_a = part_y[0][:, None] - col_map[0][None, :]
        delta_b = part_y[1][:, None] - col_map[1][None, :]
        return (jnp.where(itself, 0.0, 1.0 / (1.0 + delta_a * delta_a + delta_b * delta_b)), part_y)

    def sweep(step_fn, init):

        def wrapped(carry, index):
            return step_fn(carry, index * block_rows)

        carry, result = lax.scan(wrapped, init, jnp.arange(blocks, dtype=jnp.int32))
        return (carry, result.transpose(1, 0, 2).reshape(result.shape[1], rows_total))

    def nearest_step(carry, start):
        distance, itself = distances(start)
        masked = jnp.where(itself, jnp.inf, distance)
        return (carry, jnp.min(masked, axis=1)[None])

    col_min_part, row_min_part = sweep(nearest_step, jnp.full((cols_total,), jnp.inf, jnp.float32))
    nearest_rows = lax.pmin(row_min_part[0], "col")

    def moment_step(carry, start):
        distance, itself = distances(start)
        shifted = distance - slice_rows(nearest_rows, start)[:, None]
        expo = jnp.where(itself, 0.0, jnp.exp(-slice_rows(row_prec, start)[:, None] * shifted))
        row_part = jnp.stack(
            [
                jnp.sum(expo, axis=1),
                jnp.sum(expo * shifted, axis=1),
                jnp.sum(expo * shifted * shifted, axis=1),
            ]
        )
        return (carry, row_part)

    col_moment, row_moment = sweep(moment_step, jnp.zeros((3, cols_total), jnp.float32))
    row_z, row_first, row_second = lax.psum((row_moment[0], row_moment[1], row_moment[2]), "col")
    calib_rows = newton_update(row_z, row_first, row_second, row_prec)

    def norm_step(carry, start):
        distance, itself = distances(start)
        shifted = distance - slice_rows(nearest_rows, start)[:, None]
        row_part = jnp.sum(
            jnp.where(itself, 0.0, jnp.exp(-slice_rows(calib_rows, start)[:, None] * shifted)),
            axis=1,
        )
        return (carry, row_part[None])

    col_norm_part, row_norm_part = sweep(norm_step, jnp.zeros((cols_total,), jnp.float32))
    norm_rows = lax.psum(row_norm_part[0], "col")
    own_stats = jnp.stack(
        [
            lax.dynamic_slice_in_dim(calib_rows, own_start, per_dev, 0),
            lax.dynamic_slice_in_dim(nearest_rows, own_start, per_dev, 0),
            lax.dynamic_slice_in_dim(norm_rows, own_start, per_dev, 0),
        ]
    )
    col_stats = lax.all_gather(own_stats, "row", axis=1, tiled=True)
    calib_cols = col_stats[0]
    nearest_cols = col_stats[1]
    norm_cols = col_stats[2]

    def kernel_step(carry, index):
        start = index * block_rows
        itself = slice_rows(row_ids, start)[:, None] == col_ids[None, :]
        kernel, part_y = kernel_of(start, itself)
        return (carry + jnp.sum(kernel), None)

    kernel_part, unused = lax.scan(
        kernel_step, jnp.zeros((), jnp.float32), jnp.arange(blocks, dtype=jnp.int32)
    )
    qsum = lax.psum(kernel_part, ("row", "col"))

    def pulled(coef, part_y):
        moved = lax.dot_general(
            col_map,
            coef,
            (((1,), (1,)), ((), ())),
            precision=lax.Precision.HIGHEST,
            preferred_element_type=jnp.float32,
        )
        return part_y * jnp.sum(coef, axis=1)[None, :] - moved

    def force_step(carry, start):
        distance, itself = distances(start)
        kernel, part_y = kernel_of(start, itself)
        cond_rows = (
            jnp.exp(
                -slice_rows(calib_rows, start)[:, None]
                * (distance - slice_rows(nearest_rows, start)[:, None])
            )
            / slice_rows(norm_rows, start)[:, None]
        )
        cond_cols = (
            jnp.exp(-calib_cols[None, :] * (distance - nearest_cols[None, :])) / norm_cols[None, :]
        )
        affinity = jnp.where(itself, 0.0, 0.5 * (cond_rows + cond_cols))
        coef = (affinity - total * kernel / qsum) * kernel
        return (carry, pulled(coef, part_y))

    kernel_late, force_rows = sweep(force_step, jnp.zeros((), jnp.float32))
    force = lax.psum_scatter(force_rows, "col", scatter_dimension=1, tiled=True)
    calibrated = lax.dynamic_slice_in_dim(calib_rows, own_start, per_dev, 0)
    return (force, calibrated)


def solution(mesh):
    in_specs = (P(None, ("row", "col")), P(None, ("row", "col")), P(("row", "col")))
    out_specs = (P(None, ("row", "col")), P(("row", "col")))
    return jax.shard_map(body, mesh=mesh, in_specs=in_specs, out_specs=out_specs, check_vma=False)
```

profile of v0, /device:TPU:32, one launch (start us, length us, event | category | flops | bytes accessed | tf_op | source)
XLA Modules:
  0.0 629.3 jit_solution(9365061002655801085)
XLA Ops:
  7.2 0.8 pad_maximum_fusion
  8.0 43.2 %all_gather.9 = f32[67,2048]{1,0:T(8,128)S(1)} all-gather(f32[67,128]{1,0:T(8,128)S(1)} %pad_maximum_fusion), channel_id=1, replica_groups=mesh['row'=16,'col'=16] {'col'}, dimensions={1}, use_global_device_ids=true | all-gather | bytes 583168 | tf_op jit(solution)/shard_map/all_gather | solution.py:26
  51.2 34.5 %all_gather.10 = f32[67,2048]{1,0:T(8,128)S(1)} all-gather(f32[67,128]{1,0:T(8,128)S(1)} %pad_maximum_fusion), channel_id=1, replica_groups=mesh['row'=16,'col'=16] {'row'}, dimensions={1}, use_global_device_ids=true | all-gather | bytes 583168 | tf_op jit(solution)/shard_map/all_gather | solution.py:27
  86.5 31.0 %while.57 = (s32[]{:T(128)}, f32[8,1,256]{2,1,0:T(1,128)S(1)}, s32[8]{0:T(128)S(1)}, s32[2048]{0:T(1024)S(1)}, f32[2048]{0:T(1024)S(1)}, /*index=5*/f32[2048]{0:...) while((s32[]{:T(128)}, f32[8,1,256]{2,1,0:T(1,128)S(1)}, ...), condition=%wide.region_4.5_spmd.clone, body=%wide.region_2.4_spmd.clone.sunk | while | flops 406353664 | bytes 623819 | solution.py:74
  88.0 2.3 fusion.130
  91.8 2.3 fusion.130
  95.7 2.3 fusion.130
  99.6 2.3 fusion.130
  103.5 2.3 fusion.130
  107.4 2.3 fusion.130
  111.2 2.3 fusion.130
  115.1 2.3 fusion.130
  117.4 42.5 %pmin.7 = f32[2048]{0:T(1024)S(1)} all-reduce(f32[2048]{0:T(1024)S(1)} %bitcast.134), channel_id=1, replica_groups=mesh['row'=16,'col'=16] {'col'}, use_global_device_ids=true, to_apply=%region_5.6 | all-reduce | flops 2048 | bytes 16384 | tf_op jit(solution)/shard_map/pmin | solution.py:83
  159.9 35.0 %while.58 = (s32[]{:T(128)}, f32[8,3,256]{2,1,0:T(4,128)S(1)}, s32[8]{0:T(128)S(1)}, s32[2048]{0:T(1024)S(1)}, f32[2048]{0:T(1024)S(1)}, /*index=5*/f32[2048]{0:...) while((s32[]{:T(128)}, f32[8,3,256]{2,1,0:T(4,128)S(1)}, ...), condition=%wide.region_10.11_spmd.clone, body=%wide.region_6.10_spmd.clone.sunk | while | flops 409500672 | bytes 637155 | solution.py:74
  161.4 2.9 fusion.133
  165.8 2.9 fusion.133
  170.1 2.9 fusion.133
  174.5 2.9 fusion.133
  178.9 2.9 fusion.133
  183.3 2.9 fusion.133
  187.6 2.9 fusion.133
  192.0 2.9 fusion.133
  195.0 70.5 %all-reduce = (f32[2048]{0:T(1024)S(1)}, f32[2048]{0:T(1024)S(1)}, f32[2048]{0:T(1024)S(1)}) all-reduce(f32[2048]{0:T(1024)S(1)} %bitcast.132, f32[2048]{0:T(1024)S(1)} %bitcast.133, f32[2048]{0:T(1024)S(1)} %bitcast.131), channel_id=1, replica_groups=mesh['row'=16,'col'=16] {'col'}, use_global_device_ids=true, to_apply=%region_12.13 | all-reduce | flops 6144 | bytes 49152 | tf_op jit(solution)/shard_map/psum | solution.py:99
  265.6 33.4 %while.59 = (s32[]{:T(128)}, f32[8,1,256]{2,1,0:T(1,128)S(1)}, s32[8]{0:T(128)S(1)}, s32[2048]{0:T(1024)S(1)}, f32[2048]{0:T(1024)S(1)}, /*index=5*/f32[2048]{0:...) while((s32[]{:T(128)}, f32[8,1,256]{2,1,0:T(1,128)S(1)}, ...), condition=%wide.region_16.17_spmd.clone, body=%wide.region_14.16_spmd.clone.sunk | while | flops 407402496 | bytes 629987 | solution.py:74
  267.2 2.6 fusion.138
  271.4 2.6 fusion.138
  275.6 2.6 fusion.138
  279.7 2.6 fusion.138
  283.9 2.6 fusion.138
  288.1 2.6 fusion.138
  292.3 2.6 fusion.138
  296.4 2.6 fusion.138
  299.0 44.6 %psum.38 = f32[2048]{0:T(1024)S(1)} all-reduce(f32[2048]{0:T(1024)S(1)} %bitcast.135), channel_id=1, replica_groups=mesh['row'=16,'col'=16] {'col'}, use_global_device_ids=true, to_apply=%region_17.18 | all-reduce | flops 2048 | bytes 16384 | tf_op jit(solution)/shard_map/psum | solution.py:112
  343.7 23.8 %all_gather.11 = f32[3,2048]{1,0:T(4,128)S(1)} all-gather(f32[3,128]{1,0:T(4,128)S(1)} %pad_maximum_fusion.1), channel_id=1, replica_groups=mesh['row'=16,'col'=16] {'row'}, dimensions={1}, use_global_device_ids=true | all-gather | bytes 26112 | tf_op jit(solution)/shard_map/all_gather | solution.py:120
  367.6 34.7 %while.60 = (s32[]{:T(128)}, f32[]{:T(128)}, s32[8]{0:T(128)S(1)}, s32[2048]{0:T(1024)S(1)}, f32[2,2048]{1,0:T(2,128)S(1)}, /*index=5*/f32[2,2048]{1,0:T(2,128)S...) while((s32[]{:T(128)}, f32[]{:T(128)}, s32[8]{0:T(128)S(1)}, ...), condition=%wide.region_20.21_spmd.clone, body=%wide.region_18.20_spmd.clone.sunk | while | flops 5273607 | bytes 74971 | solution.py:131
  369.2 2.1 select_reduce_fusion.2
  373.5 2.1 select_reduce_fusion.2
  377.9 2.1 select_reduce_fusion.2
  382.2 2.1 select_reduce_fusion.2
  386.6 2.1 select_reduce_fusion.2
  390.9 2.1 select_reduce_fusion.2
  395.2 2.1 select_reduce_fusion.2
  399.6 2.1 select_reduce_fusion.2
  402.4 74.2 %psum.39 = f32[]{:T(128)} all-reduce(f32[]{:T(128)} %get-tuple-element.407), channel_id=1, replica_groups=mesh['row'=16,'col'=16] {'row','col'}, use_global_device_ids=true, to_apply=%region_21.22 | all-reduce | flops 1 | bytes 8 | tf_op jit(solution)/shard_map/psum | solution.py:134
  476.6 65.5 %while.61 = (s32[]{:T(128)}, f32[8,2,256]{2,1,0:T(2,128)S(1)}, s32[8]{0:T(128)S(1)}, f32[2,2048]{1,0:T(2,128)S(1)}, s32[2048]{0:T(1024)S(1)}, /*index=5*/f32[204...) while((s32[]{:T(128)}, f32[8,2,256]{2,1,0:T(2,128)S(1)}, ...), condition=%wide.region_24.25_spmd.clone, body=%wide.region_22.24_spmd.clone.sunk | while | flops 429423616 | bytes 4926787 | solution.py:74
  478.4 4.6 fusion.146
  483.0 1.7 fusion.147
  486.6 4.6 fusion.146
  491.2 1.7 fusion.147
  494.8 4.6 fusion.146
  499.4 1.7 fusion.147
  503.0 4.6 fusion.146
  507.6 1.7 fusion.147
  511.2 4.6 fusion.146
  515.8 1.7 fusion.147
  519.4 4.6 fusion.146
  524.0 1.7 fusion.147
  527.6 4.6 fusion.146
  532.1 1.7 fusion.147
  535.7 4.6 fusion.146
  540.3 1.7 fusion.147
  542.1 1.4 copy.8
  544.1 77.0 %reduce-scatter.4.cloned.1.call-done = f32[128,2]{1,0:T(8,128)} async-done(((f32[2048,2]{1,0:T(8,128)}), f32[128,2]{1,0:T(8,128)}) %reduce-scatter.4.cloned.1.call-update) | async-done | bytes 1040
  621.0 1.5 copy.9
  (295 shorter events, 39.0 us)
Async XLA Ops:
  7.2 613.8 %reduce-scatter.4.cloned.1.call-start = ((), (), s32[]{:S(2)}) async-start(), calls=%async_computation.1 | async-start | bytes 1114112
  51.2 34.7 %copy-start.1 = (f32[67,2048]{1,0:T(8,128)}, f32[67,2048]{1,0:T(8,128)S(1)}, u32[]{:S(2)}) copy-start(f32[67,2048]{1,0:T(8,128)S(1)} %all_gather.9) | copy-start | bytes 1646596
  85.6 0.8 copy-start
  265.6 102.0 %slice-start = ((f32[67,2048]{1,0:T(8,128)}), f32[2,2048]{1,0:T(2,128)S(1)}, s32[]{:S(2)}) async-start(f32[67,2048]{1,0:T(8,128)} %copy-done), calls=%async_computation.2 | async-start | bytes 32768 | tf_op jit(solution)/shard_map/slice | solution.py:34
  265.6 102.0 %slice-start.1 = ((f32[67,2048]{1,0:T(8,128)}), f32[2,2048]{1,0:T(2,128)S(1)}, s32[]{:S(2)}) async-start(f32[67,2048]{1,0:T(8,128)} %copy-done.1), calls=%async_computation.3 | async-start | bytes 32768 | tf_op jit(solution)/shard_map/slice | solution.py:33
Sparse Core Ops, SparseCore 0:
  543.6 77.3 reduce-scatter.3
where the time goes:
time: 635 us; the launch traced here: 629 us
  blocking collectives  333 us (52%)
  matrix products  113 us (18%)
  waiting for transfers between devices  77 us (12%)
  local copies, waits for them, and re-layouts  39.3 us (6%)
  loops' own time  32.9 us (5%)
  other arithmetic  19.9 us (3%)
  between operations  14.2 us (2%)
    dot_general x32, matrix products, distances(): lax.dot_general(part, col_coords, (((0,), (0,)), ((), ())), precision=lax...  98.8 us
    unnamed x2, waiting for transfers between devices  77 us
    psum x1, blocking collectives, body(): qsum = lax.psum(kernel_part, ('row', 'col'))  74.2 us
    psum x1, blocking collectives, body(): lax.psum((row_moment[0], row_moment[1], row_moment[2]), 'col')  70.5 us
    psum x1, blocking collectives, body(): norm_rows = lax.psum(row_norm_part[0], 'col')  44.6 us
    all_gather x1, blocking collectives, body(): row_pack = lax.all_gather(packed, 'col', axis=1, tiled=True)  43.2 us
    pmin x1, blocking collectives, body(): nearest_rows = lax.pmin(row_min_part[0], 'col')  42.5 us
    all_gather x1, blocking collectives, body(): col_pack = lax.all_gather(packed, 'row', axis=1, tiled=True)  34.5 us
  transfers between devices with their start and end apart: 1, of which 1 were waited for; matrix products, arithmetic and copies ran while one was open for 0% of the time, Pallas kernels for 0%

commit v1 on v0

v1 whole, which is shorter than its diff:
```python
import math

import jax
import jax.numpy as jnp
from jax import lax
from jax.sharding import PartitionSpec as P

PERP = 30


def newton_update(zsum, first, second, start_prec):
    entropy = jnp.log(zsum) + start_prec * first / zsum
    spread = second / zsum - (first / zsum) ** 2
    factor = jnp.clip(
        (entropy - math.log(PERP)) / jnp.maximum(start_prec * start_prec * spread, 1.0), -2.0, 2.0
    )
    return start_prec * jnp.exp(factor)


def body(points, embedding, precision):
    per_dev = points.shape[1]
    width = points.shape[0]
    axes = ("row", "col")
    me = lax.axis_index("row") * lax.axis_size("col") + lax.axis_index("col")
    own_start = me * per_dev

    packed = jnp.concatenate([points, embedding], axis=0)
    every = lax.all_gather(packed, axes, axis=1, tiled=True)
    total = every.shape[1]
    all_coords = every[:width]
    all_map = every[width : width + 2]

    own_coords = points
    own_map = embedding
    own_sq = jnp.sum(own_coords * own_coords, axis=0)
    all_sq = jnp.sum(all_coords * all_coords, axis=0)

    inner = lax.dot_general(
        own_coords,
        all_coords,
        (((0,), (0,)), ((), ())),
        precision=lax.Precision.HIGHEST,
        preferred_element_type=jnp.float32,
    )
    distance = jnp.maximum(own_sq[:, None] + all_sq[None, :] - 2.0 * inner, 0.0)
    col_ids = jnp.arange(total, dtype=jnp.int32)[None, :]
    row_ids = (own_start + jnp.arange(per_dev, dtype=jnp.int32))[:, None]
    itself = row_ids == col_ids

    nearest = jnp.min(jnp.where(itself, jnp.inf, distance), axis=1)
    shifted = distance - nearest[:, None]
    expo = jnp.where(itself, 0.0, jnp.exp(-precision[:, None] * shifted))
    zsum = jnp.sum(expo, axis=1)
    first = jnp.sum(expo * shifted, axis=1)
    second = jnp.sum(expo * shifted * shifted, axis=1)
    calib = newton_update(zsum, first, second, precision)

    norm = jnp.sum(jnp.where(itself, 0.0, jnp.exp(-calib[:, None] * shifted)), axis=1)

    delta_a = own_map[0][:, None] - all_map[0][None, :]
    delta_b = own_map[1][:, None] - all_map[1][None, :]
    kernel = jnp.where(itself, 0.0, 1.0 / (1.0 + delta_a * delta_a + delta_b * delta_b))
    kernel_part = jnp.sum(kernel)

    qslot = jnp.where(jnp.arange(per_dev) == 0, kernel_part, 0.0)
    stats = jnp.stack([calib, nearest, 1.0 / norm, qslot])
    all_stats = lax.all_gather(stats, axes, axis=1, tiled=True)
    calib_cols = all_stats[0]
    nearest_cols = all_stats[1]
    inv_norm_cols = all_stats[2]
    qsum = jnp.sum(all_stats[3])

    cond_rows = jnp.exp(-calib[:, None] * shifted) * (1.0 / norm)[:, None]
    cond_cols = (
        jnp.exp(-calib_cols[None, :] * (distance - nearest_cols[None, :])) * inv_norm_cols[None, :]
    )
    affinity = jnp.where(itself, 0.0, 0.5 * (cond_rows + cond_cols))
    coef = (affinity - total * kernel / qsum) * kernel
    force = jnp.stack([jnp.sum(coef * delta_a, axis=1), jnp.sum(coef * delta_b, axis=1)])
    return (force, calib)


def solution(mesh):
    in_specs = (P(None, ("row", "col")), P(None, ("row", "col")), P(("row", "col")))
    out_specs = (P(None, ("row", "col")), P(("row", "col")))
    return jax.shard_map(body, mesh=mesh, in_specs=in_specs, out_specs=out_specs, check_vma=False)
```

time: 635 us -> 1310 us (2.06)
  waiting for transfers between devices: 77 us -> 568 us
  blocking collectives: 333 us -> 623 us
  matrix products: 113 us -> 40.5 us
  other arithmetic: 19.9 us -> 57.2 us
  local copies, waits for them, and re-layouts: 39.3 us -> 2.68 us
  loops' own time: 32.9 us -> 0 us
    all_gather x0 -> x1, waiting for transfers between devices: none -> 568 us  [body(): every = lax.all_gather(packed, axes, axis=1, tiled=True)]
    all_gather x3 -> x1, blocking collectives: 101 us -> 623 us  [body(): all_stats = lax.all_gather(stats, axes, axis=1, tiled=True)]
    psum x3 -> x0, blocking collectives: 189 us -> none  [the longest x1 74.2 us: body(): qsum = lax.psum(kernel_part, ('row', 'col'))]
    unnamed x2 -> x1, waiting for transfers between devices: 77 us -> 0.02 us
    dot_general x40 -> x1, matrix products: 113 us -> 40.5 us  [body(): lax.dot_general(own_coords, all_coords, (((0,), (0,)), ((), ())), precisi...]
    pmin x1 -> x0, blocking collectives: 42.5 us -> none  [body(): nearest_rows = lax.pmin(row_min_part[0], 'col')]
    reduce_sum x8 -> x5, other arithmetic: 16.6 us -> 52.9 us  [the longest x1 23.7 us: body(): jnp.sum(coef * delta_a, axis=1)]
    dynamic_slice x145 -> x0, local copies, waits for them, and re-layouts: 33.9 us -> none  [the longest x40 25.5 us: sweep(): carry, result = lax.scan(wrapped, init, jnp.arange(blocks, dtype=jnp.int32))]
where the time goes in v1:
time: 1310 us
  blocking collectives  623 us (48%)
  waiting for transfers between devices  568 us (43%)
  other arithmetic  57.2 us (4%)
  matrix products  40.5 us (3%)
  between operations  14.1 us (1%)
    all_gather x1, blocking collectives, body(): all_stats = lax.all_gather(stats, axes, axis=1, tiled=True)  623 us
    all_gather x1, waiting for transfers between devices, body(): every = lax.all_gather(packed, axes, axis=1, tiled=True)  568 us
    dot_general x1, matrix products, body(): lax.dot_general(own_coords, all_coords, (((0,), (0,)), ((), ())), precisi...  40.5 us
  transfers between devices with their start and end apart: 1, of which 1 were waited for; matrix products, arithmetic and copies ran while one was open for 0% of the time, Pallas kernels for 0%

profile of v1, /device:TPU:32, one launch (start us, length us, event | category | flops | bytes accessed | tf_op | source)
XLA Modules:
  0.0 1305.3 jit_solution(480047436654380983)
XLA Ops:
  7.2 0.0 all-gather.2.cloned.1.call-start
  7.2 1.4 pad_maximum_fusion
  8.6 0.0 all-gather.2.cloned.1.call-update
  8.6 0.7 neg.12
  9.3 0.8 multiply_reduce_fusion.2
  10.1 0.8 slice_bitcast_fusion.1
  10.8 568.2 %all-gather.2.cloned.1.call-done = f32[66,32768]{1,0:T(8,128)} async-done(((f32[66,128]{1,0:T(8,128)}), f32[66,32768]{1,0:T(8,128)}) %all-gather.2.cloned.1.call-update) | async-done | bytes 8650768 | tf_op jit(solution)/shard_map/all_gather | solution.py:28
  579.0 4.2 multiply_reduce_fusion.1
  583.1 40.5 %select_reduce_fusion.1 = (f32[128]{0:T(128)S(1)}, f32[128,32768]{0,1:T(8,128)S(1)}) fusion(s32[128]{0:T(128)S(1)} %iota_add_fusion, f32[64,128]{1,0:T(8,128)} %param.3, f32[66,32768]{1,0:T(8,128)} %all-gather.2.cloned.1.call-done, f32[32768]{0:T(1024)S(1)} %multiply_reduce_fusion.1, f32[128]{0:T(128)S(1)} %multiply_reduce_fusion.2), kind=kOutput, calls=%fused_computation.22 | convolution fusion | flops 3250585600 | bytes 25331200 | tf_op jit(solution)/shard_map/dot_general | solution.py:38
  623.7 0.0 copy-start.1
  623.7 6.6 multiply_reduce_fusion
  630.2 0.0 copy-done.1
  630.3 0.0 copy-start
  630.3 1.9 fusion.15
  632.2 17.8 %select_reduce_fusion = (f32[128]{0:T(128)S(1)}, f32[]{:T(128)}) fusion(f32[128,32768]{0,1:T(8,128)S(1)} %get-tuple-element.20, f32[128]{0:T(128)S(1)} %get-tuple-element.9, f32[128]{0:T(128)S(1)} %get-tuple-element.19, s32[128]{0:T(128)S(1)} %iota_add_fusion, f32[32768]{0:T(1024)S(1)} %bitcast.24, f32[128]{0:T(128)S(1)} %get-tuple-element.18, ...), kind=kLoop, calls=%fused_computation.15 | loop fusion | flops 58720128 | bytes 17042436 | tf_op jit(solution)/shard_map/reduce_sum | solution.py:58
  650.0 0.7 compare_select_fusion
  650.7 622.6 %all_gather.7 = f32[4,32768]{1,0:T(4,128)S(1)} all-gather(f32[4,128]{1,0:T(4,128)S(1)} %pad_maximum_fusion.1), channel_id=1, replica_groups=mesh['row'=16,'col'=16] {'row','col'}, dimensions={1}, use_global_device_ids=true | all-gather | bytes 526336 | tf_op jit(solution)/shard_map/all_gather | solution.py:67
  1273.3 1.0 slice_negate_fusion
  1274.2 23.7 %fusion.7 = (f32[128]{0:T(128)S(1)}, f32[128]{0:T(128)S(1)}) fusion(f32[32768]{0:T(1024)S(1)} %bitcast.23, f32[128]{0:T(128)S(1)} %get-tuple-element.17, f32[32768]{0:T(1024)S(1)} %bitcast.25, f32[128]{0:T(128)S(1)} %get-tuple-element.18, f32[]{:T(128)} %get-tuple-element.14, f32[32768]{0:T(1024)S(1)} %bitcast.27, f32[128,32768]{0,1:T(8,128)S(1)} %get-tuple-element.20, ...), kind=kLoop, calls=%fused_computation.12 | loop fusion | flops 109051648 | bytes 17436676 | tf_op jit(solution)/shard_map/reduce_sum | solution.py:79
  1297.9 0.0 copy-done
  1297.9 0.6 pad_maximum_fusion.2
  (5 shorter events, 0.0 us)
Async XLA Ops:
  7.2 571.8 %all-gather.2.cloned.1.call-start = ((), (), s32[]{:S(2)}) async-start(), calls=%async_computation | async-start | bytes 9474048 | tf_op jit(solution)/shard_map/all_gather | solution.py:28
  623.7 6.6 copy-start.1
  630.3 667.6 %copy-start = (f32[128]{0:T(128)}, f32[128]{0:T(128)S(1)}, u32[]{:S(2)}) copy-start(f32[128]{0:T(128)S(1)} %get-tuple-element.10) | copy-start | bytes 1540
Sparse Core Ops, SparseCore 0:
  9.8 569.1 all-gather.1

commit v2 on v1

--- a/solution.py
+++ b/solution.py
@@ -25,7 +25,7 @@
     own_start = me * per_dev
 
     packed = jnp.concatenate([points, embedding], axis=0)
-    every = lax.all_gather(packed, axes, axis=1, tiled=True)
+    every = lax.all_gather(lax.all_gather(packed, "col", axis=1, tiled=True), "row", axis=1, tiled=True)
     total = every.shape[1]
     all_coords = every[:width]
     all_map = every[width : width + 2]
@@ -64,7 +64,7 @@
 
     qslot = jnp.where(jnp.arange(per_dev) == 0, kernel_part, 0.0)
     stats = jnp.stack([calib, nearest, 1.0 / norm, qslot])
-    all_stats = lax.all_gather(stats, axes, axis=1, tiled=True)
+    all_stats = lax.all_gather(lax.all_gather(stats, "col", axis=1, tiled=True), "row", axis=1, tiled=True)
     calib_cols = all_stats[0]
     nearest_cols = all_stats[1]
     inv_norm_cols = all_stats[2]

time: 1310 us -> 343 us (0.26)
  blocking collectives: 623 us -> 110 us
  waiting for transfers between devices: 568 us -> 116 us
    all_gather x1 -> x3, blocking collectives: 623 us -> 110 us  [the longest x1 45.8 us: body(): lax.all_gather(packed, 'col', axis=1, tiled=True)]
    all_gather x1, waiting for transfers between devices: 568 us -> 116 us  [body(): lax.all_gather(lax.all_gather(packed, 'col', axis=1, tiled=True), 'row',...]
  transfers between devices with their start and end apart: 1 -> 1, of which waited for: 1 -> 1; matrix products, arithmetic and copies ran while one was open for 0% -> 1% of each run, Pallas kernels for 0% -> 0%
where the time goes in v2:
time: 343 us; the launch traced here: 340 us
  waiting for transfers between devices  116 us (34%)
  blocking collectives  110 us (32%)
  other arithmetic  56.6 us (17%)
  matrix products  40.5 us (12%)
  between operations  14.1 us (4%)
    all_gather x1, waiting for transfers between devices, body(): lax.all_gather(lax.all_gather(packed, 'col', axis=1, tiled=True), 'row',...  116 us
    all_gather x1, blocking collectives, body(): lax.all_gather(packed, 'col', axis=1, tiled=True)  45.8 us
    dot_general x1, matrix products, body(): lax.dot_general(own_coords, all_coords, (((0,), (0,)), ((), ())), precisi...  40.5 us
    all_gather x1, blocking collectives, body(): lax.all_gather(stats, 'col', axis=1, tiled=True)  38.4 us
    all_gather x1, blocking collectives, body(): lax.all_gather(lax.all_gather(stats, 'col', axis=1, tiled=True), 'row', a...  25.8 us
    reduce_sum x1, other arithmetic, body(): jnp.sum(coef * delta_a, axis=1)  23.7 us
    reduce_sum x1, other arithmetic, body(): jnp.sum(jnp.where(itself, 0.0, jnp.exp(-calib[:, None] * shifted)), axis=1)  17.8 us
  transfers between devices with their start and end apart: 1, of which 1 were waited for; matrix products, arithmetic and copies ran while one was open for 1% of the time, Pallas kernels for 0%

profile of v2, /device:TPU:32, one launch (start us, length us, event | category | flops | bytes accessed | tf_op | source)
XLA Modules:
  0.0 340.1 jit_solution(15328813931579001438)
XLA Ops:
  7.2 0.0 all-gather.2.cloned.1.call-start
  7.2 0.8 pad_maximum_fusion
  8.0 45.8 %all_gather.12 = f32[66,2048]{1,0:T(8,128)} all-gather(f32[66,128]{1,0:T(8,128)S(1)} %pad_maximum_fusion), channel_id=1, replica_groups=mesh['row'=16,'col'=16] {'col'}, dimensions={1}, use_global_device_ids=true | all-gather | bytes 574464 | tf_op jit(solution)/shard_map/all_gather | solution.py:28
  53.8 0.0 all-gather.2.cloned.1.call-update
  53.8 0.7 neg.12
  54.5 0.8 multiply_reduce_fusion.2
  55.3 0.8 slice_bitcast_fusion.1
  56.0 116.1 %all-gather.2.cloned.1.call-done = f32[66,32768]{1,0:T(8,128)} async-done(((f32[66,2048]{1,0:T(8,128)}), f32[66,32768]{1,0:T(8,128)}) %all-gather.2.cloned.1.call-update) | async-done | bytes 8650768 | tf_op jit(solution)/shard_map/all_gather | solution.py:28
  172.1 4.2 %multiply_reduce_fusion.1 = f32[32768]{0:T(1024)S(1)} fusion(f32[66,32768]{1,0:T(8,128)} %all-gather.2.cloned.1.call-done), kind=kLoop, calls=%fused_computation.24 | loop fusion | flops 4161536 | bytes 8519680 | tf_op jit(solution)/shard_map/reduce_sum | solution.py:36
  176.3 40.5 %select_reduce_fusion.1 = (f32[128]{0:T(128)S(1)}, f32[128,32768]{0,1:T(8,128)S(1)}) fusion(s32[128]{0:T(128)S(1)} %iota_add_fusion, f32[64,128]{1,0:T(8,128)} %param.3, f32[66,32768]{1,0:T(8,128)} %all-gather.2.cloned.1.call-done, f32[32768]{0:T(1024)S(1)} %multiply_reduce_fusion.1, f32[128]{0:T(128)S(1)} %multiply_reduce_fusion.2), kind=kOutput, calls=%fused_computation.22 | convolution fusion | flops 3250585600 | bytes 25331200 | tf_op jit(solution)/shard_map/dot_general | solution.py:38
  216.8 0.0 copy-start.1
  216.8 6.6 %multiply_reduce_fusion = (f32[128]{0:T(128)S(1)}, f32[128]{0:T(128)S(1)}, f32[128]{0:T(128)S(1)}) fusion(f32[128,32768]{0,1:T(8,128)S(1)} %get-tuple-element.20, f32[128]{0:T(128)S(1)} %get-tuple-element.19, f32[128]{0:T(128)S(1)} %neg.12, s32[128]{0:T(128)S(1)} %iota_add_fusion), kind=kLoop, calls=%fused_computation.17 | loop fusion | flops 37748352 | bytes 16780288 | tf_op jit(solution)/shard_map/reduce_sum | solution.py:55
  223.4 0.0 copy-done.1
  223.4 0.0 copy-start
  223.4 1.9 fusion.15
  225.4 17.8 %select_reduce_fusion = (f32[128]{0:T(128)S(1)}, f32[]{:T(128)}) fusion(f32[128,32768]{0,1:T(8,128)S(1)} %get-tuple-element.20, f32[128]{0:T(128)S(1)} %get-tuple-element.9, f32[128]{0:T(128)S(1)} %get-tuple-element.19, s32[128]{0:T(128)S(1)} %iota_add_fusion, f32[32768]{0:T(1024)S(1)} %bitcast.24, f32[128]{0:T(128)S(1)} %get-tuple-element.18, ...), kind=kLoop, calls=%fused_computation.15 | loop fusion | flops 58720128 | bytes 17042436 | tf_op jit(solution)/shard_map/reduce_sum | solution.py:58
  243.1 0.7 compare_select_fusion
  243.8 38.4 %all_gather.14 = f32[4,2048]{1,0:T(4,128)S(1)} all-gather(f32[4,128]{1,0:T(4,128)S(1)} %pad_maximum_fusion.1), channel_id=1, replica_groups=mesh['row'=16,'col'=16] {'col'}, dimensions={1}, use_global_device_ids=true | all-gather | bytes 34816 | tf_op jit(solution)/shard_map/all_gather | solution.py:67
  282.3 25.8 %all_gather.15 = f32[4,32768]{1,0:T(4,128)S(1)} all-gather(f32[4,2048]{1,0:T(4,128)S(1)} %all_gather.14), channel_id=1, replica_groups=mesh['row'=16,'col'=16] {'row'}, dimensions={1}, use_global_device_ids=true | all-gather | bytes 557056 | tf_op jit(solution)/shard_map/all_gather | solution.py:67
  308.1 1.0 slice_negate_fusion
  309.0 23.7 %fusion.7 = (f32[128]{0:T(128)S(1)}, f32[128]{0:T(128)S(1)}) fusion(f32[32768]{0:T(1024)S(1)} %bitcast.23, f32[128]{0:T(128)S(1)} %get-tuple-element.17, f32[32768]{0:T(1024)S(1)} %bitcast.25, f32[128]{0:T(128)S(1)} %get-tuple-element.18, f32[]{:T(128)} %get-tuple-element.14, f32[32768]{0:T(1024)S(1)} %bitcast.27, f32[128,32768]{0,1:T(8,128)S(1)} %get-tuple-element.20, ...), kind=kLoop, calls=%fused_computation.12 | loop fusion | flops 109051648 | bytes 17436676 | tf_op jit(solution)/shard_map/reduce_sum | solution.py:79
  332.7 0.0 copy-done
  332.7 0.6 pad_maximum_fusion.2
  (5 shorter events, 0.0 us)
Async XLA Ops:
  7.2 165.0 %all-gather.2.cloned.1.call-start = ((), (), s32[]{:S(2)}) async-start(), calls=%async_computation | async-start | bytes 10027008 | tf_op jit(solution)/shard_map/all_gather | solution.py:28
  216.8 6.6 %copy-start.1 = (f32[128]{0:T(128)S(1)}, f32[128]{0:T(128)}, u32[]{:S(2)}) copy-start(f32[128]{0:T(128)} %param.5) | copy-start | bytes 1540
  223.4 109.3 %copy-start = (f32[128]{0:T(128)}, f32[128]{0:T(128)S(1)}, u32[]{:S(2)}) copy-start(f32[128]{0:T(128)S(1)} %get-tuple-element.10) | copy-start | bytes 1540
Sparse Core Ops, SparseCore 0:
  53.9 118.1 all-gather.1

commit v3 on v2

--- a/solution.py
+++ b/solution.py
@@ -17,23 +17,34 @@
     return start_prec * jnp.exp(factor)
 
 
+def col_stage(values):
+    count = lax.axis_size("col")
+    parts = [values]
+    for shift in range(1, count):
+        pairs = [(i, (i + shift) % count) for i in range(count)]
+        parts.append(lax.ppermute(values, "col", pairs))
+    return jnp.concatenate(parts, axis=1)
+
+
+def spread_all(values):
+    return lax.all_gather(col_stage(values), "row", axis=1, tiled=True)
+
+
 def body(points, embedding, precision):
     per_dev = points.shape[1]
     width = points.shape[0]
     axes = ("row", "col")
-    me = lax.axis_index("row") * lax.axis_size("col") + lax.axis_index("col")
-    own_start = me * per_dev
-
-    packed = jnp.concatenate([points, embedding], axis=0)
-    every = lax.all_gather(lax.all_gather(packed, "col", axis=1, tiled=True), "row", axis=1, tiled=True)
-    total = every.shape[1]
-    all_coords = every[:width]
-    all_map = every[width : width + 2]
+    own_start = lax.axis_index("row") * lax.axis_size("col") * per_dev
 
     own_coords = points
     own_map = embedding
     own_sq = jnp.sum(own_coords * own_coords, axis=0)
-    all_sq = jnp.sum(all_coords * all_coords, axis=0)
+    packed = jnp.concatenate([points, embedding, own_sq[None, :]], axis=0)
+    every = spread_all(packed)
+    total = every.shape[1]
+    all_coords = every[:width]
+    all_map = every[width : width + 2]
+    all_sq = every[width + 2]
 
     inner = lax.dot_general(
         own_coords,
@@ -64,7 +75,7 @@
 
     qslot = jnp.where(jnp.arange(per_dev) == 0, kernel_part, 0.0)
     stats = jnp.stack([calib, nearest, 1.0 / norm, qslot])
-    all_stats = lax.all_gather(lax.all_gather(stats, "col", axis=1, tiled=True), "row", axis=1, tiled=True)
+    all_stats = spread_all(stats)
     calib_cols = all_stats[0]
     nearest_cols = all_stats[1]
     inv_norm_cols = all_stats[2]

time: 343 us -> 335 us (0.977)
  blocking collectives: 110 us -> 27.2 us
  starting transfers between devices: 0.04 us -> 59 us
  matrix products: 40.5 us -> 49.5 us
  waiting for transfers between devices: 116 us -> 122 us
  other arithmetic: 56.6 us -> 52.5 us
    all_gather x3 -> x1, blocking collectives: 110 us -> 27.2 us  [spread_all(): return lax.all_gather(col_stage(values), 'row', axis=1, tiled=True)]
    ppermute x0 -> x30, starting transfers between devices: none -> 58.9 us  [col_stage(): parts.append(lax.ppermute(values, 'col', pairs))]
    dot_general x1, matrix products: 40.5 us -> 49.5 us  [body(): lax.dot_general(own_coords, all_coords, (((0,), (0,)), ((), ())), precisi...]
    ppermute x0 -> x30, waiting for transfers between devices: none -> 7.42 us  [col_stage(): parts.append(lax.ppermute(values, 'col', pairs))]
    reduce_sum x1 -> x0, other arithmetic: 4.16 us -> none  [body(): all_sq = jnp.sum(all_coords * all_coords, axis=0)]
  transfers between devices with their start and end apart: 1 -> 31, of which waited for: 1 -> 5; matrix products, arithmetic and copies ran while one was open for 1% -> 0% of each run, Pallas kernels for 0% -> 0%
where the time goes in v3:
time: 335 us; the launch traced here: 329 us
  waiting for transfers between devices  122 us (36%)
  starting transfers between devices  59 us (18%)
  other arithmetic  52.5 us (16%)
  matrix products  49.5 us (15%)
  blocking collectives  27.2 us (8%)
  between operations  14.5 us (4%)
  local copies, waits for them, and re-layouts  4.3 us (1%)
    all_gather x1, waiting for transfers between devices, spread_all(): return lax.all_gather(col_stage(values), 'row', axis=1, tiled=True)  115 us
    ppermute x30, starting transfers between devices, col_stage(): parts.append(lax.ppermute(values, 'col', pairs))  58.9 us
    dot_general x1, matrix products, body(): lax.dot_general(own_coords, all_coords, (((0,), (0,)), ((), ())), precisi...  49.5 us
    all_gather x1, blocking collectives, spread_all(): return lax.all_gather(col_stage(values), 'row', axis=1, tiled=True)  27.2 us
    reduce_sum x1, other arithmetic, body(): jnp.sum(coef * delta_a, axis=1)  23.7 us
    reduce_sum x1, other arithmetic, body(): jnp.sum(jnp.where(itself, 0.0, jnp.exp(-calib[:, None] * shifted)), axis=1)  17.8 us
    ppermute x30, waiting for transfers between devices, col_stage(): parts.append(lax.ppermute(values, 'col', pairs))  7.42 us
  transfers between devices with their start and end apart: 31, of which 5 were waited for; matrix products, arithmetic and copies ran while one was open for 0% of the time, Pallas kernels for 0%

profile of v3, /device:TPU:32, one launch (start us, length us, event | category | flops | bytes accessed | tf_op | source)
XLA Modules:
  0.0 329.4 jit_solution(3125415079185128367)
XLA Ops:
  7.2 0.0 all-gather.2.cloned.1.call-start
  7.2 0.8 multiply_reduce_fusion.1
  8.0 0.8 pad_maximum_fusion
  8.8 1.9 collective-permute-start
  10.7 1.6 collective-permute-start.1
  12.3 2.8 collective-permute-start.2
  15.1 1.6 collective-permute-start.3
  16.7 1.3 collective-permute-start.4
  17.9 0.0 collective-permute-done
  17.9 3.5 %collective-permute-start.5 = (f32[67,128]{1,0:T(8,128)S(1)}, f32[67,128]{1,0:T(8,128)S(1)}, u32[]{:S(2)}, u32[]{:S(2)}) collective-permute-start(f32[67,128]{1,0:T(8,128)S(1)} %get-tuple-element.18), channel_id=1, source_target_pairs={{0,6},{1,7},{2,8},{3,9},{4,10},{5,11},{6,12},{7,13},{8,14},{9,15},... | collective-permute-start | bytes 102920 | tf_op jit(solution)/shard_map/ppermute | solution.py:25
  21.4 0.0 collective-permute-done.1
  21.4 0.6 collective-permute-start.6
  22.1 0.0 collective-permute-done.2
  22.1 2.4 collective-permute-start.7
  24.5 4.3 %collective-permute-start.8 = (f32[67,128]{1,0:T(8,128)S(1)}, f32[67,128]{1,0:T(8,128)S(1)}, u32[]{:S(2)}, u32[]{:S(2)}) collective-permute-start(f32[67,128]{1,0:T(8,128)S(1)} %get-tuple-element.18), channel_id=1, source_target_pairs={{0,9},{1,10},{2,11},{3,12},{4,13},{5,14},{6,15},{7,0},{8,1},{9,2},... | collective-permute-start | bytes 102920 | tf_op jit(solution)/shard_map/ppermute | solution.py:25
  28.8 0.0 collective-permute-done.4
  28.8 1.3 collective-permute-start.9
  30.1 0.0 collective-permute-done.5
  30.1 1.4 collective-permute-start.10
  31.6 1.2 collective-permute-start.11
  32.8 0.0 collective-permute-done.7
  32.8 1.0 collective-permute-start.12
  33.8 5.0 %collective-permute-start.13 = (f32[67,128]{1,0:T(8,128)S(1)}, f32[67,128]{1,0:T(8,128)S(1)}, u32[]{:S(2)}, u32[]{:S(2)}) collective-permute-start(f32[67,128]{1,0:T(8,128)S(1)} %get-tuple-element.18), channel_id=1, source_target_pairs={{0,14},{1,15},{2,0},{3,1},{4,2},{5,3},{6,4},{7,5},{8,6},{9,7},{10,... | collective-permute-start | bytes 102920 | tf_op jit(solution)/shard_map/ppermute | solution.py:25
  38.8 0.0 collective-permute-start.14
  38.8 0.0 collective-permute-done.12
  38.9 2.6 collective-permute-done.13
  41.5 1.3 collective-permute-done.14
  42.7 0.8 copy-done
  43.6 0.0 all-gather.2.cloned.1.call-update
  43.6 0.7 neg.12
  44.2 0.8 slice_bitcast_fusion.1
  45.0 115.0 %all-gather.2.cloned.1.call-done = f32[67,32768]{1,0:T(8,128)} async-done(((f32[67,2048]{1,0:T(8,128)}), f32[67,32768]{1,0:T(8,128)}) %all-gather.2.cloned.1.call-update) | async-done | bytes 8781840 | tf_op jit(solution)/shard_map/all_gather | solution.py:30
  160.0 2.5 fusion.15
  162.6 49.5 %select_reduce_fusion.1 = (f32[128]{0:T(128)S(1)}, f32[128,32768]{0,1:T(8,128)S(1)}) fusion(s32[128]{0:T(128)S(1)} %iota_add_fusion, f32[64,128]{1,0:T(8,128)} %param.3, f32[67,32768]{1,0:T(8,128)} %all-gather.2.cloned.1.call-done, f32[32768]{0:T(1024)S(1)} %bitcast.31, f32[128]{0:T(128)S(1)} %multiply_reduce_fusion.1), kind=kOutput, calls=%fused_computation.22 | convolution fusion | flops 3250585600 | bytes 25331200 | tf_op jit(solution)/shard_map/dot_general | solution.py:49
  212.1 0.0 copy-start.2
  212.1 6.6 %multiply_reduce_fusion = (f32[128]{0:T(128)S(1)}, f32[128]{0:T(128)S(1)}, f32[128]{0:T(128)S(1)}) fusion(f32[128,32768]{0,1:T(8,128)S(1)} %get-tuple-element.25, f32[128]{0:T(128)S(1)} %get-tuple-element.24, f32[128]{0:T(128)S(1)} %neg.12, s32[128]{0:T(128)S(1)} %iota_add_fusion), kind=kLoop, calls=%fused_computation.17 | loop fusion | flops 37748352 | bytes 16780288 | tf_op jit(solution)/shard_map/reduce_sum | solution.py:66
  218.7 0.0 copy-start.1
  218.7 17.8 %select_reduce_fusion = (f32[128]{0:T(128)S(1)}, f32[]{:T(128)}) fusion(f32[128,32768]{0,1:T(8,128)S(1)} %get-tuple-element.25, f32[128]{0:T(128)S(1)} %get-tuple-element.9, f32[128]{0:T(128)S(1)} %get-tuple-element.24, s32[128]{0:T(128)S(1)} %iota_add_fusion, f32[32768]{0:T(1024)S(1)} %bitcast.26, f32[128]{0:T(128)S(1)} %get-tuple-element.23, ...), kind=kLoop, calls=%fused_computation.15 | loop fusion | flops 58720128 | bytes 17042436 | tf_op jit(solution)/shard_map/reduce_sum | solution.py:69
  236.5 0.6 compare_select_fusion
  237.2 0.2 collective-permute-start.15
  237.4 4.7 %collective-permute-start.16 = (f32[4,128]{1,0:T(4,128)S(1)}, f32[4,128]{1,0:T(4,128)S(1)}, u32[]{:S(2)}, u32[]{:S(2)}) collective-permute-start(f32[4,128]{1,0:T(4,128)S(1)} %get-tuple-element.20), channel_id=1, source_target_pairs={{0,2},{1,3},{2,4},{3,5},{4,6},{5,7},{6,8},{7,9},{8,10},{9,11},{10,... | collective-permute-start | bytes 6152 | tf_op jit(solution)/shard_map/ppermute | solution.py:25
  242.1 0.0 collective-permute-start.17
  242.1 1.5 collective-permute-start.18
  243.6 2.6 collective-permute-start.19
  246.1 0.0 collective-permute-done.15
  246.1 2.7 collective-permute-start.20
  248.9 1.4 collective-permute-start.21
  250.3 1.4 collective-permute-start.22
  251.7 0.0 collective-permute-done.18
  251.7 4.3 %collective-permute-start.23 = (f32[4,128]{1,0:T(4,128)S(1)}, f32[4,128]{1,0:T(4,128)S(1)}, u32[]{:S(2)}, u32[]{:S(2)}) collective-permute-start(f32[4,128]{1,0:T(4,128)S(1)} %get-tuple-element.20), channel_id=1, source_target_pairs={{0,9},{1,10},{2,11},{3,12},{4,13},{5,14},{6,15},{7,0},{8,1},{9,2},... | collective-permute-start | bytes 6152 | tf_op jit(solution)/shard_map/ppermute | solution.py:25
  256.1 0.0 collective-permute-done.19
  256.1 3.8 %collective-permute-start.24 = (f32[4,128]{1,0:T(4,128)S(1)}, f32[4,128]{1,0:T(4,128)S(1)}, u32[]{:S(2)}, u32[]{:S(2)}) collective-permute-start(f32[4,128]{1,0:T(4,128)S(1)} %get-tuple-element.20), channel_id=1, source_target_pairs={{0,10},{1,11},{2,12},{3,13},{4,14},{5,15},{6,0},{7,1},{8,2},{9,3},... | collective-permute-start | bytes 6152 | tf_op jit(solution)/shard_map/ppermute | solution.py:25
  259.9 1.2 collective-permute-start.26
  261.1 0.0 collective-permute-done.22
  261.1 1.9 collective-permute-start.27
  263.0 3.3 collective-permute-start.28
  266.3 0.0 collective-permute-done.24
  266.3 0.0 collective-permute-done.26
  266.4 1.8 collective-permute-done.28
  268.2 1.7 collective-permute-done.29
  269.9 27.2 %all_gather.7 = f32[4,32768]{1,0:T(4,128)S(1)} all-gather(f32[4,2048]{1,0:T(4,128)S(1)} %constant_dynamic-update-slice_fusion.16), channel_id=1, replica_groups=mesh['row'=16,'col'=16] {'row'}, dimensions={1}, use_global_device_ids=true | all-gather | bytes 557056 | tf_op jit(solution)/shard_map/all_gather | solution.py:30
  297.1 1.0 slice_negate_fusion
  298.1 23.7 %fusion.7 = (f32[128]{0:T(128)S(1)}, f32[128]{0:T(128)S(1)}) fusion(f32[32768]{0:T(1024)S(1)} %bitcast.25, f32[128]{0:T(128)S(1)} %get-tuple-element.22, f32[32768]{0:T(1024)S(1)} %bitcast.27, f32[128]{0:T(128)S(1)} %get-tuple-element.23, f32[]{:T(128)} %get-tuple-element.15, f32[32768]{0:T(1024)S(1)} %bitcast.29, f32[128,32768]{0,1:T(8,128)S(1)} %get-tuple-element.25, ...), kind=kLoop, calls=%fused_computation.12 | loop fusion | flops 109051648 | bytes 17436676 | tf_op jit(solution)/shard_map/reduce_sum | solution.py:90
  321.8 0.6 pad_maximum_fusion.2
  (53 shorter events, 0.3 us)
Async XLA Ops:
  7.2 152.9 %all-gather.2.cloned.1.call-start = ((), (), s32[]{:S(2)}) async-start(), calls=%async_computation | async-start | bytes 10027008 | tf_op jit(solution)/shard_map/all_gather | solution.py:30
  8.8 9.2 %collective-permute-start = (f32[67,128]{1,0:T(8,128)S(1)}, f32[67,128]{1,0:T(8,128)S(1)}, u32[]{:S(2)}, u32[]{:S(2)}) collective-permute-start(f32[67,128]{1,0:T(8,128)S(1)} %get-tuple-element.18), channel_id=1, source_target_pairs={{0,1},{1,2},{2,3},{3,4},{4,5},{5,6},{6,7},{7,8},{8,9},{9,10},{10,1... | collective-permute-start | bytes 102920 | tf_op jit(solution)/shard_map/ppermute | solution.py:25
  10.7 10.7 %collective-permute-start.1 = (f32[67,128]{1,0:T(8,128)S(1)}, f32[67,128]{1,0:T(8,128)S(1)}, u32[]{:S(2)}, u32[]{:S(2)}) collective-permute-start(f32[67,128]{1,0:T(8,128)S(1)} %get-tuple-element.18), channel_id=1, source_target_pairs={{0,2},{1,3},{2,4},{3,5},{4,6},{5,7},{6,8},{7,9},{8,10},{9,11},{10,... | collective-permute-start | bytes 102920 | tf_op jit(solution)/shard_map/ppermute | solution.py:25
  12.3 9.8 %collective-permute-start.2 = (f32[67,128]{1,0:T(8,128)S(1)}, f32[67,128]{1,0:T(8,128)S(1)}, u32[]{:S(2)}, u32[]{:S(2)}) collective-permute-start(f32[67,128]{1,0:T(8,128)S(1)} %get-tuple-element.18), channel_id=1, source_target_pairs={{0,3},{1,4},{2,5},{3,6},{4,7},{5,8},{6,9},{7,10},{8,11},{9,12},{10... | collective-permute-start | bytes 102920 | tf_op jit(solution)/shard_map/ppermute | solution.py:25
  15.1 9.4 %collective-permute-start.3 = (f32[67,128]{1,0:T(8,128)S(1)}, f32[67,128]{1,0:T(8,128)S(1)}, u32[]{:S(2)}, u32[]{:S(2)}) collective-permute-start(f32[67,128]{1,0:T(8,128)S(1)} %get-tuple-element.18), channel_id=1, source_target_pairs={{0,4},{1,5},{2,6},{3,7},{4,8},{5,9},{6,10},{7,11},{8,12},{9,13},{1... | collective-permute-start | bytes 102920 | tf_op jit(solution)/shard_map/ppermute | solution.py:25
  16.7 12.1 %collective-permute-start.4 = (f32[67,128]{1,0:T(8,128)S(1)}, f32[67,128]{1,0:T(8,128)S(1)}, u32[]{:S(2)}, u32[]{:S(2)}) collective-permute-start(f32[67,128]{1,0:T(8,128)S(1)} %get-tuple-element.18), channel_id=1, source_target_pairs={{0,5},{1,6},{2,7},{3,8},{4,9},{5,10},{6,11},{7,12},{8,13},{9,14},{... | collective-permute-start | bytes 102920 | tf_op jit(solution)/shard_map/ppermute | solution.py:25
  17.9 12.2 %collective-permute-start.5 = (f32[67,128]{1,0:T(8,128)S(1)}, f32[67,128]{1,0:T(8,128)S(1)}, u32[]{:S(2)}, u32[]{:S(2)}) collective-permute-start(f32[67,128]{1,0:T(8,128)S(1)} %get-tuple-element.18), channel_id=1, source_target_pairs={{0,6},{1,7},{2,8},{3,9},{4,10},{5,11},{6,12},{7,13},{8,14},{9,15},... | collective-permute-start | bytes 102920 | tf_op jit(solution)/shard_map/ppermute | solution.py:25
  21.4 10.1 %collective-permute-start.6 = (f32[67,128]{1,0:T(8,128)S(1)}, f32[67,128]{1,0:T(8,128)S(1)}, u32[]{:S(2)}, u32[]{:S(2)}) collective-permute-start(f32[67,128]{1,0:T(8,128)S(1)} %get-tuple-element.18), channel_id=1, source_target_pairs={{0,7},{1,8},{2,9},{3,10},{4,11},{5,12},{6,13},{7,14},{8,15},{9,0},... | collective-permute-start | bytes 102920 | tf_op jit(solution)/shard_map/ppermute | solution.py:25
  22.1 10.7 %collective-permute-start.7 = (f32[67,128]{1,0:T(8,128)S(1)}, f32[67,128]{1,0:T(8,128)S(1)}, u32[]{:S(2)}, u32[]{:S(2)}) collective-permute-start(f32[67,128]{1,0:T(8,128)S(1)} %get-tuple-element.18), channel_id=1, source_target_pairs={{0,8},{1,9},{2,10},{3,11},{4,12},{5,13},{6,14},{7,15},{8,0},{9,1},... | collective-permute-start | bytes 102920 | tf_op jit(solution)/shard_map/ppermute | solution.py:25
  24.5 9.3 %collective-permute-start.8 = (f32[67,128]{1,0:T(8,128)S(1)}, f32[67,128]{1,0:T(8,128)S(1)}, u32[]{:S(2)}, u32[]{:S(2)}) collective-permute-start(f32[67,128]{1,0:T(8,128)S(1)} %get-tuple-element.18), channel_id=1, source_target_pairs={{0,9},{1,10},{2,11},{3,12},{4,13},{5,14},{6,15},{7,0},{8,1},{9,2},... | collective-permute-start | bytes 102920 | tf_op jit(solution)/shard_map/ppermute | solution.py:25
  28.8 10.0 %collective-permute-start.9 = (f32[67,128]{1,0:T(8,128)S(1)}, f32[67,128]{1,0:T(8,128)S(1)}, u32[]{:S(2)}, u32[]{:S(2)}) collective-permute-start(f32[67,128]{1,0:T(8,128)S(1)} %get-tuple-element.18), channel_id=1, source_target_pairs={{0,10},{1,11},{2,12},{3,13},{4,14},{5,15},{6,0},{7,1},{8,2},{9,3},... | collective-permute-start | bytes 102920 | tf_op jit(solution)/shard_map/ppermute | solution.py:25
  30.1 8.7 %collective-permute-start.10 = (f32[67,128]{1,0:T(8,128)S(1)}, f32[67,128]{1,0:T(8,128)S(1)}, u32[]{:S(2)}, u32[]{:S(2)}) collective-permute-start(f32[67,128]{1,0:T(8,128)S(1)} %get-tuple-element.18), channel_id=1, source_target_pairs={{0,11},{1,12},{2,13},{3,14},{4,15},{5,0},{6,1},{7,2},{8,3},{9,4},{... | collective-permute-start | bytes 102920 | tf_op jit(solution)/shard_map/ppermute | solution.py:25
  31.6 7.3 %collective-permute-start.11 = (f32[67,128]{1,0:T(8,128)S(1)}, f32[67,128]{1,0:T(8,128)S(1)}, u32[]{:S(2)}, u32[]{:S(2)}) collective-permute-start(f32[67,128]{1,0:T(8,128)S(1)} %get-tuple-element.18), channel_id=1, source_target_pairs={{0,12},{1,13},{2,14},{3,15},{4,0},{5,1},{6,2},{7,3},{8,4},{9,5},{1... | collective-permute-start | bytes 102920 | tf_op jit(solution)/shard_map/ppermute | solution.py:25
  32.8 6.1 %collective-permute-start.12 = (f32[67,128]{1,0:T(8,128)S(1)}, f32[67,128]{1,0:T(8,128)S(1)}, u32[]{:S(2)}, u32[]{:S(2)}) collective-permute-start(f32[67,128]{1,0:T(8,128)S(1)} %get-tuple-element.18), channel_id=1, source_target_pairs={{0,13},{1,14},{2,15},{3,0},{4,1},{5,2},{6,3},{7,4},{8,5},{9,6},{10... | collective-permute-start | bytes 102920 | tf_op jit(solution)/shard_map/ppermute | solution.py:25
  33.8 7.7 %collective-permute-start.13 = (f32[67,128]{1,0:T(8,128)S(1)}, f32[67,128]{1,0:T(8,128)S(1)}, u32[]{:S(2)}, u32[]{:S(2)}) collective-permute-start(f32[67,128]{1,0:T(8,128)S(1)} %get-tuple-element.18), channel_id=1, source_target_pairs={{0,14},{1,15},{2,0},{3,1},{4,2},{5,3},{6,4},{7,5},{8,6},{9,7},{10,... | collective-permute-start | bytes 102920 | tf_op jit(solution)/shard_map/ppermute | solution.py:25
  38.8 4.0 %collective-permute-start.14 = (f32[67,128]{1,0:T(8,128)S(1)}, f32[67,128]{1,0:T(8,128)S(1)}, u32[]{:S(2)}, u32[]{:S(2)}) collective-permute-start(f32[67,128]{1,0:T(8,128)S(1)} %get-tuple-element.18), channel_id=1, source_target_pairs={{0,15},{1,0},{2,1},{3,2},{4,3},{5,4},{6,5},{7,6},{8,7},{9,8},{10,9... | collective-permute-start | bytes 102920 | tf_op jit(solution)/shard_map/ppermute | solution.py:25
  42.7 0.8 copy-start
  212.1 6.6 %copy-start.2 = (f32[128]{0:T(128)S(1)}, f32[128]{0:T(128)}, u32[]{:S(2)}) copy-start(f32[128]{0:T(128)} %param.5) | copy-start | bytes 1540
  218.7 103.0 %copy-start.1 = (f32[128]{0:T(128)}, f32[128]{0:T(128)S(1)}, u32[]{:S(2)}) copy-start(f32[128]{0:T(128)S(1)} %get-tuple-element.10) | copy-start | bytes 1540
  237.2 9.0 %collective-permute-start.15 = (f32[4,128]{1,0:T(4,128)S(1)}, f32[4,128]{1,0:T(4,128)S(1)}, u32[]{:S(2)}, u32[]{:S(2)}) collective-permute-start(f32[4,128]{1,0:T(4,128)S(1)} %get-tuple-element.20), channel_id=1, source_target_pairs={{0,1},{1,2},{2,3},{3,4},{4,5},{5,6},{6,7},{7,8},{8,9},{9,10},{10,1... | collective-permute-start | bytes 6152 | tf_op jit(solution)/shard_map/ppermute | solution.py:25
  237.4 11.5 %collective-permute-start.16 = (f32[4,128]{1,0:T(4,128)S(1)}, f32[4,128]{1,0:T(4,128)S(1)}, u32[]{:S(2)}, u32[]{:S(2)}) collective-permute-start(f32[4,128]{1,0:T(4,128)S(1)} %get-tuple-element.20), channel_id=1, source_target_pairs={{0,2},{1,3},{2,4},{3,5},{4,6},{5,7},{6,8},{7,9},{8,10},{9,11},{10,... | collective-permute-start | bytes 6152 | tf_op jit(solution)/shard_map/ppermute | solution.py:25
  242.1 8.3 %collective-permute-start.17 = (f32[4,128]{1,0:T(4,128)S(1)}, f32[4,128]{1,0:T(4,128)S(1)}, u32[]{:S(2)}, u32[]{:S(2)}) collective-permute-start(f32[4,128]{1,0:T(4,128)S(1)} %get-tuple-element.20), channel_id=1, source_target_pairs={{0,3},{1,4},{2,5},{3,6},{4,7},{5,8},{6,9},{7,10},{8,11},{9,12},{10... | collective-permute-start | bytes 6152 | tf_op jit(solution)/shard_map/ppermute | solution.py:25
  242.1 9.7 %collective-permute-start.18 = (f32[4,128]{1,0:T(4,128)S(1)}, f32[4,128]{1,0:T(4,128)S(1)}, u32[]{:S(2)}, u32[]{:S(2)}) collective-permute-start(f32[4,128]{1,0:T(4,128)S(1)} %get-tuple-element.20), channel_id=1, source_target_pairs={{0,4},{1,5},{2,6},{3,7},{4,8},{5,9},{6,10},{7,11},{8,12},{9,13},{1... | collective-permute-start | bytes 6152 | tf_op jit(solution)/shard_map/ppermute | solution.py:25
  243.6 12.5 %collective-permute-start.19 = (f32[4,128]{1,0:T(4,128)S(1)}, f32[4,128]{1,0:T(4,128)S(1)}, u32[]{:S(2)}, u32[]{:S(2)}) collective-permute-start(f32[4,128]{1,0:T(4,128)S(1)} %get-tuple-element.20), channel_id=1, source_target_pairs={{0,5},{1,6},{2,7},{3,8},{4,9},{5,10},{6,11},{7,12},{8,13},{9,14},{... | collective-permute-start | bytes 6152 | tf_op jit(solution)/shard_map/ppermute | solution.py:25
  246.1 13.7 %collective-permute-start.20 = (f32[4,128]{1,0:T(4,128)S(1)}, f32[4,128]{1,0:T(4,128)S(1)}, u32[]{:S(2)}, u32[]{:S(2)}) collective-permute-start(f32[4,128]{1,0:T(4,128)S(1)} %get-tuple-element.20), channel_id=1, source_target_pairs={{0,6},{1,7},{2,8},{3,9},{4,10},{5,11},{6,12},{7,13},{8,14},{9,15},... | collective-permute-start | bytes 6152 | tf_op jit(solution)/shard_map/ppermute | solution.py:25
  248.9 11.0 %collective-permute-start.21 = (f32[4,128]{1,0:T(4,128)S(1)}, f32[4,128]{1,0:T(4,128)S(1)}, u32[]{:S(2)}, u32[]{:S(2)}) collective-permute-start(f32[4,128]{1,0:T(4,128)S(1)} %get-tuple-element.20), channel_id=1, source_target_pairs={{0,7},{1,8},{2,9},{3,10},{4,11},{5,12},{6,13},{7,14},{8,15},{9,0},... | collective-permute-start | bytes 6152 | tf_op jit(solution)/shard_map/ppermute | solution.py:25
  250.3 10.8 %collective-permute-start.22 = (f32[4,128]{1,0:T(4,128)S(1)}, f32[4,128]{1,0:T(4,128)S(1)}, u32[]{:S(2)}, u32[]{:S(2)}) collective-permute-start(f32[4,128]{1,0:T(4,128)S(1)} %get-tuple-element.20), channel_id=1, source_target_pairs={{0,8},{1,9},{2,10},{3,11},{4,12},{5,13},{6,14},{7,15},{8,0},{9,1},... | collective-permute-start | bytes 6152 | tf_op jit(solution)/shard_map/ppermute | solution.py:25
  251.7 11.3 %collective-permute-start.23 = (f32[4,128]{1,0:T(4,128)S(1)}, f32[4,128]{1,0:T(4,128)S(1)}, u32[]{:S(2)}, u32[]{:S(2)}) collective-permute-start(f32[4,128]{1,0:T(4,128)S(1)} %get-tuple-element.20), channel_id=1, source_target_pairs={{0,9},{1,10},{2,11},{3,12},{4,13},{5,14},{6,15},{7,0},{8,1},{9,2},... | collective-permute-start | bytes 6152 | tf_op jit(solution)/shard_map/ppermute | solution.py:25
  256.1 10.2 %collective-permute-start.24 = (f32[4,128]{1,0:T(4,128)S(1)}, f32[4,128]{1,0:T(4,128)S(1)}, u32[]{:S(2)}, u32[]{:S(2)}) collective-permute-start(f32[4,128]{1,0:T(4,128)S(1)} %get-tuple-element.20), channel_id=1, source_target_pairs={{0,10},{1,11},{2,12},{3,13},{4,14},{5,15},{6,0},{7,1},{8,2},{9,3},... | collective-permute-start | bytes 6152 | tf_op jit(solution)/shard_map/ppermute | solution.py:25
  259.9 6.4 %collective-permute-start.25 = (f32[4,128]{1,0:T(4,128)S(1)}, f32[4,128]{1,0:T(4,128)S(1)}, u32[]{:S(2)}, u32[]{:S(2)}) collective-permute-start(f32[4,128]{1,0:T(4,128)S(1)} %get-tuple-element.20), channel_id=1, source_target_pairs={{0,11},{1,12},{2,13},{3,14},{4,15},{5,0},{6,1},{7,2},{8,3},{9,4},{... | collective-permute-start | bytes 6152 | tf_op jit(solution)/shard_map/ppermute | solution.py:25
  259.9 6.4 %collective-permute-start.26 = (f32[4,128]{1,0:T(4,128)S(1)}, f32[4,128]{1,0:T(4,128)S(1)}, u32[]{:S(2)}, u32[]{:S(2)}) collective-permute-start(f32[4,128]{1,0:T(4,128)S(1)} %get-tuple-element.20), channel_id=1, source_target_pairs={{0,12},{1,13},{2,14},{3,15},{4,0},{5,1},{6,2},{7,3},{8,4},{9,5},{1... | collective-permute-start | bytes 6152 | tf_op jit(solution)/shard_map/ppermute | solution.py:25
  261.1 5.2 %collective-permute-start.27 = (f32[4,128]{1,0:T(4,128)S(1)}, f32[4,128]{1,0:T(4,128)S(1)}, u32[]{:S(2)}, u32[]{:S(2)}) collective-permute-start(f32[4,128]{1,0:T(4,128)S(1)} %get-tuple-element.20), channel_id=1, source_target_pairs={{0,13},{1,14},{2,15},{3,0},{4,1},{5,2},{6,3},{7,4},{8,5},{9,6},{10... | collective-permute-start | bytes 6152 | tf_op jit(solution)/shard_map/ppermute | solution.py:25
  263.0 5.2 %collective-permute-start.28 = (f32[4,128]{1,0:T(4,128)S(1)}, f32[4,128]{1,0:T(4,128)S(1)}, u32[]{:S(2)}, u32[]{:S(2)}) collective-permute-start(f32[4,128]{1,0:T(4,128)S(1)} %get-tuple-element.20), channel_id=1, source_target_pairs={{0,14},{1,15},{2,0},{3,1},{4,2},{5,3},{6,4},{7,5},{8,6},{9,7},{10,... | collective-permute-start | bytes 6152 | tf_op jit(solution)/shard_map/ppermute | solution.py:25
  266.3 3.6 %collective-permute-start.29 = (f32[4,128]{1,0:T(4,128)S(1)}, f32[4,128]{1,0:T(4,128)S(1)}, u32[]{:S(2)}, u32[]{:S(2)}) collective-permute-start(f32[4,128]{1,0:T(4,128)S(1)} %get-tuple-element.20), channel_id=1, source_target_pairs={{0,15},{1,0},{2,1},{3,2},{4,3},{5,4},{6,5},{7,6},{8,7},{9,8},{10,9... | collective-permute-start | bytes 6152 | tf_op jit(solution)/shard_map/ppermute | solution.py:25
Sparse Core Ops, SparseCore 0:
  43.7 116.2 all-gather.1

commit v4 on v3

--- a/solution.py
+++ b/solution.py
@@ -66,12 +66,19 @@
     second = jnp.sum(expo * shifted * shifted, axis=1)
     calib = newton_update(zsum, first, second, precision)
 
-    norm = jnp.sum(jnp.where(itself, 0.0, jnp.exp(-calib[:, None] * shifted)), axis=1)
+    row_expo = jnp.where(itself, 0.0, jnp.exp(-calib[:, None] * shifted))
+    norm = jnp.sum(row_expo, axis=1)
 
     delta_a = own_map[0][:, None] - all_map[0][None, :]
     delta_b = own_map[1][:, None] - all_map[1][None, :]
     kernel = jnp.where(itself, 0.0, 1.0 / (1.0 + delta_a * delta_a + delta_b * delta_b))
     kernel_part = jnp.sum(kernel)
+    row_pull = row_expo * kernel
+    row_push = kernel * kernel
+    pull_a = jnp.sum(row_pull * delta_a, axis=1)
+    pull_b = jnp.sum(row_pull * delta_b, axis=1)
+    push_a = jnp.sum(row_push * delta_a, axis=1)
+    push_b = jnp.sum(row_push * delta_b, axis=1)
 
     qslot = jnp.where(jnp.arange(per_dev) == 0, kernel_part, 0.0)
     stats = jnp.stack([calib, nearest, 1.0 / norm, qslot])
@@ -81,13 +88,20 @@
     inv_norm_cols = all_stats[2]
     qsum = jnp.sum(all_stats[3])
 
-    cond_rows = jnp.exp(-calib[:, None] * shifted) * (1.0 / norm)[:, None]
     cond_cols = (
         jnp.exp(-calib_cols[None, :] * (distance - nearest_cols[None, :])) * inv_norm_cols[None, :]
     )
-    affinity = jnp.where(itself, 0.0, 0.5 * (cond_rows + cond_cols))
-    coef = (affinity - total * kernel / qsum) * kernel
-    force = jnp.stack([jnp.sum(coef * delta_a, axis=1), jnp.sum(coef * delta_b, axis=1)])
+    col_pull = jnp.where(itself, 0.0, cond_cols) * kernel
+    col_a = jnp.sum(col_pull * delta_a, axis=1)
+    col_b = jnp.sum(col_pull * delta_b, axis=1)
+    half_inv = 0.5 / norm
+    scale = total / qsum
+    force = jnp.stack(
+        [
+            half_inv * pull_a + 0.5 * col_a - scale * push_a,
+            half_inv * pull_b + 0.5 * col_b - scale * push_b,
+        ]
+    )
     return (force, calib)
 
 

time: 335 us -> 338 us (level)
    reduce_sum x2 -> x3, other arithmetic: 41.4 us -> 44.7 us  [the longest x1 25.5 us: body(): col_a = jnp.sum(col_pull * delta_a, axis=1)]
where the time goes in v4:
time: 338 us; the launch traced here: 332 us
  waiting for transfers between devices  122 us (36%)
  starting transfers between devices  58.9 us (17%)
  other arithmetic  54.8 us (16%)
  matrix products  49.6 us (15%)
  blocking collectives  27.2 us (8%)
  between operations  15.2 us (4%)
  local copies, waits for them, and re-layouts  4.31 us (1%)
    all_gather x1, waiting for transfers between devices, spread_all(): return lax.all_gather(col_stage(values), 'row', axis=1, tiled=True)  115 us
    ppermute x30, starting transfers between devices, col_stage(): parts.append(lax.ppermute(values, 'col', pairs))  58.9 us
    dot_general x1, matrix products, body(): lax.dot_general(own_coords, all_coords, (((0,), (0,)), ((), ())), precisi...  49.6 us
    all_gather x1, blocking collectives, spread_all(): return lax.all_gather(col_stage(values), 'row', axis=1, tiled=True)  27.2 us
    reduce_sum x1, other arithmetic, body(): col_a = jnp.sum(col_pull * delta_a, axis=1)  25.5 us
    reduce_sum x1, other arithmetic, body(): pull_a = jnp.sum(row_pull * delta_a, axis=1)  18.3 us
    ppermute x30, waiting for transfers between devices, col_stage(): parts.append(lax.ppermute(values, 'col', pairs))  7.42 us
  transfers between devices with their start and end apart: 31, of which 5 were waited for; matrix products, arithmetic and copies ran while one was open for 0% of the time, Pallas kernels for 0%

profile of v4, /device:TPU:32, one launch (start us, length us, event | category | flops | bytes accessed | tf_op | source)
XLA Modules:
  0.0 332.5 jit_solution(17968102106806906190)
XLA Ops:
  7.2 0.0 all-gather.2.cloned.1.call-start
  7.2 0.8 multiply_reduce_fusion.1
  8.0 0.8 pad_maximum_fusion
  8.8 1.9 collective-permute-start
  10.7 1.6 collective-permute-start.1
  12.3 2.8 collective-permute-start.2
  15.1 1.6 collective-permute-start.3
  16.7 1.3 collective-permute-start.4
  17.9 0.0 collective-permute-done
  17.9 3.5 %collective-permute-start.5 = (f32[67,128]{1,0:T(8,128)S(1)}, f32[67,128]{1,0:T(8,128)S(1)}, u32[]{:S(2)}, u32[]{:S(2)}) collective-permute-start(f32[67,128]{1,0:T(8,128)S(1)} %get-tuple-element.22), channel_id=1, source_target_pairs={{0,6},{1,7},{2,8},{3,9},{4,10},{5,11},{6,12},{7,13},{8,14},{9,15},... | collective-permute-start | bytes 102920 | tf_op jit(solution)/shard_map/ppermute | solution.py:25
  21.4 0.0 collective-permute-done.1
  21.4 0.6 collective-permute-start.6
  22.1 0.0 collective-permute-done.2
  22.1 2.4 collective-permute-start.7
  24.5 4.3 %collective-permute-start.8 = (f32[67,128]{1,0:T(8,128)S(1)}, f32[67,128]{1,0:T(8,128)S(1)}, u32[]{:S(2)}, u32[]{:S(2)}) collective-permute-start(f32[67,128]{1,0:T(8,128)S(1)} %get-tuple-element.22), channel_id=1, source_target_pairs={{0,9},{1,10},{2,11},{3,12},{4,13},{5,14},{6,15},{7,0},{8,1},{9,2},... | collective-permute-start | bytes 102920 | tf_op jit(solution)/shard_map/ppermute | solution.py:25
  28.8 0.0 collective-permute-done.4
  28.8 1.3 collective-permute-start.9
  30.1 0.0 collective-permute-done.5
  30.1 1.4 collective-permute-start.10
  31.6 1.2 collective-permute-start.11
  32.8 0.0 collective-permute-done.7
  32.8 1.0 collective-permute-start.12
  33.8 5.0 %collective-permute-start.13 = (f32[67,128]{1,0:T(8,128)S(1)}, f32[67,128]{1,0:T(8,128)S(1)}, u32[]{:S(2)}, u32[]{:S(2)}) collective-permute-start(f32[67,128]{1,0:T(8,128)S(1)} %get-tuple-element.22), channel_id=1, source_target_pairs={{0,14},{1,15},{2,0},{3,1},{4,2},{5,3},{6,4},{7,5},{8,6},{9,7},{10,... | collective-permute-start | bytes 102920 | tf_op jit(solution)/shard_map/ppermute | solution.py:25
  38.8 0.0 collective-permute-start.14
  38.8 0.0 collective-permute-done.12
  38.9 2.6 collective-permute-done.13
  41.5 1.3 collective-permute-done.14
  42.7 0.8 copy-done.1
  43.6 0.0 all-gather.2.cloned.1.call-update
  43.6 0.7 neg.11
  44.2 0.8 slice_bitcast_fusion
  45.0 115.0 %all-gather.2.cloned.1.call-done = f32[67,32768]{1,0:T(8,128)} async-done(((f32[67,2048]{1,0:T(8,128)}), f32[67,32768]{1,0:T(8,128)}) %all-gather.2.cloned.1.call-update) | async-done | bytes 8781840 | tf_op jit(solution)/shard_map/all_gather | solution.py:30
  160.0 2.5 fusion.21
  162.6 49.6 %select_reduce_fusion = (f32[128]{0:T(128)S(1)}, f32[128,32768]{0,1:T(8,128)S(1)}) fusion(s32[128]{0:T(128)S(1)} %iota_add_fusion, f32[64,128]{1,0:T(8,128)} %param.3, f32[67,32768]{1,0:T(8,128)} %all-gather.2.cloned.1.call-done, f32[32768]{0:T(1024)S(1)} %bitcast.33, f32[128]{0:T(128)S(1)} %multiply_reduce_fusion.1), kind=kOutput, calls=%fused_computation.29 | convolution fusion | flops 3250585600 | bytes 25331200 | tf_op jit(solution)/shard_map/dot_general | solution.py:49
  212.1 0.0 copy-start.3
  212.2 6.6 %multiply_reduce_fusion = (f32[128]{0:T(128)S(1)}, f32[128]{0:T(128)S(1)}, f32[128]{0:T(128)S(1)}) fusion(f32[128,32768]{0,1:T(8,128)S(1)} %get-tuple-element.31, f32[128]{0:T(128)S(1)} %get-tuple-element.30, f32[128]{0:T(128)S(1)} %neg.11, s32[128]{0:T(128)S(1)} %iota_add_fusion), kind=kLoop, calls=%fused_computation.24 | loop fusion | flops 37748352 | bytes 16780288 | tf_op jit(solution)/shard_map/reduce_sum | solution.py:66
  218.8 0.0 copy-start.2
  218.8 18.3 %fusion.7 = (f32[128]{0:T(128)S(1)}, f32[128]{0:T(128)S(1)}, f32[128]{0:T(128)S(1)}, f32[]{:T(128)}, f32[128]{0:T(128)S(1)}, /*index=5*/f32[128]{0:T(128)S(1)}) fusion(f32[32768]{0:T(1024)S(1)} %bitcast.28, f32[128]{0:T(128)S(1)} %get-tuple-element.27, f32[32768]{0:T(1024)S(1)} %bitcast.26, f32[128]{0:T(128)S(1)} %get-tuple-element.26, ...), kind=kLoop, calls=%fused_computation.16 | loop fusion | flops 100662656 | bytes 17044484 | tf_op jit(solution)/shard_map/reduce_sum | solution.py:78
  237.0 0.6 compare_select_fusion
  237.7 0.2 collective-permute-start.15
  237.9 4.7 %collective-permute-start.16 = (f32[4,128]{1,0:T(4,128)S(1)}, f32[4,128]{1,0:T(4,128)S(1)}, u32[]{:S(2)}, u32[]{:S(2)}) collective-permute-start(f32[4,128]{1,0:T(4,128)S(1)} %get-tuple-element.24), channel_id=1, source_target_pairs={{0,2},{1,3},{2,4},{3,5},{4,6},{5,7},{6,8},{7,9},{8,10},{9,11},{10,... | collective-permute-start | bytes 6152 | tf_op jit(solution)/shard_map/ppermute | solution.py:25
  242.6 0.0 collective-permute-start.17
  242.6 1.5 collective-permute-start.18
  244.1 2.6 collective-permute-start.19
  246.7 0.0 collective-permute-done.15
  246.7 2.7 collective-permute-start.20
  249.4 1.4 collective-permute-start.21
  250.8 1.4 collective-permute-start.22
  252.2 4.3 %collective-permute-start.23 = (f32[4,128]{1,0:T(4,128)S(1)}, f32[4,128]{1,0:T(4,128)S(1)}, u32[]{:S(2)}, u32[]{:S(2)}) collective-permute-start(f32[4,128]{1,0:T(4,128)S(1)} %get-tuple-element.24), channel_id=1, source_target_pairs={{0,9},{1,10},{2,11},{3,12},{4,13},{5,14},{6,15},{7,0},{8,1},{9,2},... | collective-permute-start | bytes 6152 | tf_op jit(solution)/shard_map/ppermute | solution.py:25
  256.6 0.0 collective-permute-done.19
  256.6 3.8 %collective-permute-start.24 = (f32[4,128]{1,0:T(4,128)S(1)}, f32[4,128]{1,0:T(4,128)S(1)}, u32[]{:S(2)}, u32[]{:S(2)}) collective-permute-start(f32[4,128]{1,0:T(4,128)S(1)} %get-tuple-element.24), channel_id=1, source_target_pairs={{0,10},{1,11},{2,12},{3,13},{4,14},{5,15},{6,0},{7,1},{8,2},{9,3},... | collective-permute-start | bytes 6152 | tf_op jit(solution)/shard_map/ppermute | solution.py:25
  260.4 0.0 collective-permute-done.20
  260.4 1.2 collective-permute-start.26
  261.7 1.9 collective-permute-start.27
  263.5 3.3 collective-permute-start.28
  266.8 0.0 collective-permute-done.24
  266.8 0.0 collective-permute-start.29
  266.9 0.0 collective-permute-done.26
  266.9 1.8 collective-permute-done.28
  268.7 1.7 collective-permute-done.29
  270.4 27.2 %all_gather.7 = f32[4,32768]{1,0:T(4,128)S(1)} all-gather(f32[4,2048]{1,0:T(4,128)S(1)} %constant_dynamic-update-slice_fusion.16), channel_id=1, replica_groups=mesh['row'=16,'col'=16] {'row'}, dimensions={1}, use_global_device_ids=true | all-gather | bytes 557056 | tf_op jit(solution)/shard_map/all_gather | solution.py:30
  297.6 1.0 slice_reduce_fusion
  299.3 25.5 %fusion.8 = (f32[128]{0:T(128)S(1)}, f32[128]{0:T(128)S(1)}) fusion(f32[32768]{0:T(1024)S(1)} %bitcast.29, f32[128]{0:T(128)S(1)} %get-tuple-element.27, f32[32768]{0:T(1024)S(1)} %bitcast.27, f32[128]{0:T(128)S(1)} %get-tuple-element.26, f32[32768]{0:T(1024)S(1)} %bitcast.30, f32[128,32768]{0,1:T(8,128)} %copy-done, f32[32768]{0:T(1024)S(1)} %bitcast.31, ...), kind=kLoop, calls=%fused_computation.17 | loop fusion | flops 75497216 | bytes 17435136 | tf_op jit(solution)/shard_map/reduce_sum | solution.py:95
  324.8 0.6 pad_maximum_fusion.2
  (55 shorter events, 0.3 us)
Async XLA Ops:
  7.2 152.9 %all-gather.2.cloned.1.call-start = ((), (), s32[]{:S(2)}) async-start(), calls=%async_computation | async-start | bytes 10027008 | tf_op jit(solution)/shard_map/all_gather | solution.py:30
  8.8 9.2 %collective-permute-start = (f32[67,128]{1,0:T(8,128)S(1)}, f32[67,128]{1,0:T(8,128)S(1)}, u32[]{:S(2)}, u32[]{:S(2)}) collective-permute-start(f32[67,128]{1,0:T(8,128)S(1)} %get-tuple-element.22), channel_id=1, source_target_pairs={{0,1},{1,2},{2,3},{3,4},{4,5},{5,6},{6,7},{7,8},{8,9},{9,10},{10,1... | collective-permute-start | bytes 102920 | tf_op jit(solution)/shard_map/ppermute | solution.py:25
  10.7 10.7 %collective-permute-start.1 = (f32[67,128]{1,0:T(8,128)S(1)}, f32[67,128]{1,0:T(8,128)S(1)}, u32[]{:S(2)}, u32[]{:S(2)}) collective-permute-start(f32[67,128]{1,0:T(8,128)S(1)} %get-tuple-element.22), channel_id=1, source_target_pairs={{0,2},{1,3},{2,4},{3,5},{4,6},{5,7},{6,8},{7,9},{8,10},{9,11},{10,... | collective-permute-start | bytes 102920 | tf_op jit(solution)/shard_map/ppermute | solution.py:25
  12.3 9.8 %collective-permute-start.2 = (f32[67,128]{1,0:T(8,128)S(1)}, f32[67,128]{1,0:T(8,128)S(1)}, u32[]{:S(2)}, u32[]{:S(2)}) collective-permute-start(f32[67,128]{1,0:T(8,128)S(1)} %get-tuple-element.22), channel_id=1, source_target_pairs={{0,3},{1,4},{2,5},{3,6},{4,7},{5,8},{6,9},{7,10},{8,11},{9,12},{10... | collective-permute-start | bytes 102920 | tf_op jit(solution)/shard_map/ppermute | solution.py:25
  15.1 9.4 %collective-permute-start.3 = (f32[67,128]{1,0:T(8,128)S(1)}, f32[67,128]{1,0:T(8,128)S(1)}, u32[]{:S(2)}, u32[]{:S(2)}) collective-permute-start(f32[67,128]{1,0:T(8,128)S(1)} %get-tuple-element.22), channel_id=1, source_target_pairs={{0,4},{1,5},{2,6},{3,7},{4,8},{5,9},{6,10},{7,11},{8,12},{9,13},{1... | collective-permute-start | bytes 102920 | tf_op jit(solution)/shard_map/ppermute | solution.py:25
  16.7 12.1 %collective-permute-start.4 = (f32[67,128]{1,0:T(8,128)S(1)}, f32[67,128]{1,0:T(8,128)S(1)}, u32[]{:S(2)}, u32[]{:S(2)}) collective-permute-start(f32[67,128]{1,0:T(8,128)S(1)} %get-tuple-element.22), channel_id=1, source_target_pairs={{0,5},{1,6},{2,7},{3,8},{4,9},{5,10},{6,11},{7,12},{8,13},{9,14},{... | collective-permute-start | bytes 102920 | tf_op jit(solution)/shard_map/ppermute | solution.py:25
  17.9 12.2 %collective-permute-start.5 = (f32[67,128]{1,0:T(8,128)S(1)}, f32[67,128]{1,0:T(8,128)S(1)}, u32[]{:S(2)}, u32[]{:S(2)}) collective-permute-start(f32[67,128]{1,0:T(8,128)S(1)} %get-tuple-element.22), channel_id=1, source_target_pairs={{0,6},{1,7},{2,8},{3,9},{4,10},{5,11},{6,12},{7,13},{8,14},{9,15},... | collective-permute-start | bytes 102920 | tf_op jit(solution)/shard_map/ppermute | solution.py:25
  21.4 10.1 %collective-permute-start.6 = (f32[67,128]{1,0:T(8,128)S(1)}, f32[67,128]{1,0:T(8,128)S(1)}, u32[]{:S(2)}, u32[]{:S(2)}) collective-permute-start(f32[67,128]{1,0:T(8,128)S(1)} %get-tuple-element.22), channel_id=1, source_target_pairs={{0,7},{1,8},{2,9},{3,10},{4,11},{5,12},{6,13},{7,14},{8,15},{9,0},... | collective-permute-start | bytes 102920 | tf_op jit(solution)/shard_map/ppermute | solution.py:25
  22.1 10.7 %collective-permute-start.7 = (f32[67,128]{1,0:T(8,128)S(1)}, f32[67,128]{1,0:T(8,128)S(1)}, u32[]{:S(2)}, u32[]{:S(2)}) collective-permute-start(f32[67,128]{1,0:T(8,128)S(1)} %get-tuple-element.22), channel_id=1, source_target_pairs={{0,8},{1,9},{2,10},{3,11},{4,12},{5,13},{6,14},{7,15},{8,0},{9,1},... | collective-permute-start | bytes 102920 | tf_op jit(solution)/shard_map/ppermute | solution.py:25
  24.5 9.3 %collective-permute-start.8 = (f32[67,128]{1,0:T(8,128)S(1)}, f32[67,128]{1,0:T(8,128)S(1)}, u32[]{:S(2)}, u32[]{:S(2)}) collective-permute-start(f32[67,128]{1,0:T(8,128)S(1)} %get-tuple-element.22), channel_id=1, source_target_pairs={{0,9},{1,10},{2,11},{3,12},{4,13},{5,14},{6,15},{7,0},{8,1},{9,2},... | collective-permute-start | bytes 102920 | tf_op jit(solution)/shard_map/ppermute | solution.py:25
  28.8 10.0 %collective-permute-start.9 = (f32[67,128]{1,0:T(8,128)S(1)}, f32[67,128]{1,0:T(8,128)S(1)}, u32[]{:S(2)}, u32[]{:S(2)}) collective-permute-start(f32[67,128]{1,0:T(8,128)S(1)} %get-tuple-element.22), channel_id=1, source_target_pairs={{0,10},{1,11},{2,12},{3,13},{4,14},{5,15},{6,0},{7,1},{8,2},{9,3},... | collective-permute-start | bytes 102920 | tf_op jit(solution)/shard_map/ppermute | solution.py:25
  30.1 8.7 %collective-permute-start.10 = (f32[67,128]{1,0:T(8,128)S(1)}, f32[67,128]{1,0:T(8,128)S(1)}, u32[]{:S(2)}, u32[]{:S(2)}) collective-permute-start(f32[67,128]{1,0:T(8,128)S(1)} %get-tuple-element.22), channel_id=1, source_target_pairs={{0,11},{1,12},{2,13},{3,14},{4,15},{5,0},{6,1},{7,2},{8,3},{9,4},{... | collective-permute-start | bytes 102920 | tf_op jit(solution)/shard_map/ppermute | solution.py:25
  31.6 7.3 %collective-permute-start.11 = (f32[67,128]{1,0:T(8,128)S(1)}, f32[67,128]{1,0:T(8,128)S(1)}, u32[]{:S(2)}, u32[]{:S(2)}) collective-permute-start(f32[67,128]{1,0:T(8,128)S(1)} %get-tuple-element.22), channel_id=1, source_target_pairs={{0,12},{1,13},{2,14},{3,15},{4,0},{5,1},{6,2},{7,3},{8,4},{9,5},{1... | collective-permute-start | bytes 102920 | tf_op jit(solution)/shard_map/ppermute | solution.py:25
  32.8 6.1 %collective-permute-start.12 = (f32[67,128]{1,0:T(8,128)S(1)}, f32[67,128]{1,0:T(8,128)S(1)}, u32[]{:S(2)}, u32[]{:S(2)}) collective-permute-start(f32[67,128]{1,0:T(8,128)S(1)} %get-tuple-element.22), channel_id=1, source_target_pairs={{0,13},{1,14},{2,15},{3,0},{4,1},{5,2},{6,3},{7,4},{8,5},{9,6},{10... | collective-permute-start | bytes 102920 | tf_op jit(solution)/shard_map/ppermute | solution.py:25
  33.8 7.7 %collective-permute-start.13 = (f32[67,128]{1,0:T(8,128)S(1)}, f32[67,128]{1,0:T(8,128)S(1)}, u32[]{:S(2)}, u32[]{:S(2)}) collective-permute-start(f32[67,128]{1,0:T(8,128)S(1)} %get-tuple-element.22), channel_id=1, source_target_pairs={{0,14},{1,15},{2,0},{3,1},{4,2},{5,3},{6,4},{7,5},{8,6},{9,7},{10,... | collective-permute-start | bytes 102920 | tf_op jit(solution)/shard_map/ppermute | solution.py:25
  38.8 4.0 %collective-permute-start.14 = (f32[67,128]{1,0:T(8,128)S(1)}, f32[67,128]{1,0:T(8,128)S(1)}, u32[]{:S(2)}, u32[]{:S(2)}) collective-permute-start(f32[67,128]{1,0:T(8,128)S(1)} %get-tuple-element.22), channel_id=1, source_target_pairs={{0,15},{1,0},{2,1},{3,2},{4,3},{5,4},{6,5},{7,6},{8,7},{9,8},{10,9... | collective-permute-start | bytes 102920 | tf_op jit(solution)/shard_map/ppermute | solution.py:25
  42.7 0.8 copy-start.1
  212.1 24.9 %copy-start = (f32[128,32768]{0,1:T(8,128)}, f32[128,32768]{0,1:T(8,128)S(1)}, u32[]{:S(2)}) copy-start(f32[128,32768]{0,1:T(8,128)S(1)} %get-tuple-element.31) | copy-start | bytes 50331652
  212.1 6.6 %copy-start.3 = (f32[128]{0:T(128)S(1)}, f32[128]{0:T(128)}, u32[]{:S(2)}) copy-start(f32[128]{0:T(128)} %param.5) | copy-start | bytes 1540
  218.8 106.0 %copy-start.2 = (f32[128]{0:T(128)}, f32[128]{0:T(128)S(1)}, u32[]{:S(2)}) copy-start(f32[128]{0:T(128)S(1)} %get-tuple-element.14) | copy-start | bytes 1540
  237.7 9.0 %collective-permute-start.15 = (f32[4,128]{1,0:T(4,128)S(1)}, f32[4,128]{1,0:T(4,128)S(1)}, u32[]{:S(2)}, u32[]{:S(2)}) collective-permute-start(f32[4,128]{1,0:T(4,128)S(1)} %get-tuple-element.24), channel_id=1, source_target_pairs={{0,1},{1,2},{2,3},{3,4},{4,5},{5,6},{6,7},{7,8},{8,9},{9,10},{10,1... | collective-permute-start | bytes 6152 | tf_op jit(solution)/shard_map/ppermute | solution.py:25
  237.9 11.5 %collective-permute-start.16 = (f32[4,128]{1,0:T(4,128)S(1)}, f32[4,128]{1,0:T(4,128)S(1)}, u32[]{:S(2)}, u32[]{:S(2)}) collective-permute-start(f32[4,128]{1,0:T(4,128)S(1)} %get-tuple-element.24), channel_id=1, source_target_pairs={{0,2},{1,3},{2,4},{3,5},{4,6},{5,7},{6,8},{7,9},{8,10},{9,11},{10,... | collective-permute-start | bytes 6152 | tf_op jit(solution)/shard_map/ppermute | solution.py:25
  242.6 8.3 %collective-permute-start.17 = (f32[4,128]{1,0:T(4,128)S(1)}, f32[4,128]{1,0:T(4,128)S(1)}, u32[]{:S(2)}, u32[]{:S(2)}) collective-permute-start(f32[4,128]{1,0:T(4,128)S(1)} %get-tuple-element.24), channel_id=1, source_target_pairs={{0,3},{1,4},{2,5},{3,6},{4,7},{5,8},{6,9},{7,10},{8,11},{9,12},{10... | collective-permute-start | bytes 6152 | tf_op jit(solution)/shard_map/ppermute | solution.py:25
  242.6 9.7 %collective-permute-start.18 = (f32[4,128]{1,0:T(4,128)S(1)}, f32[4,128]{1,0:T(4,128)S(1)}, u32[]{:S(2)}, u32[]{:S(2)}) collective-permute-start(f32[4,128]{1,0:T(4,128)S(1)} %get-tuple-element.24), channel_id=1, source_target_pairs={{0,4},{1,5},{2,6},{3,7},{4,8},{5,9},{6,10},{7,11},{8,12},{9,13},{1... | collective-permute-start | bytes 6152 | tf_op jit(solution)/shard_map/ppermute | solution.py:25
  244.1 12.5 %collective-permute-start.19 = (f32[4,128]{1,0:T(4,128)S(1)}, f32[4,128]{1,0:T(4,128)S(1)}, u32[]{:S(2)}, u32[]{:S(2)}) collective-permute-start(f32[4,128]{1,0:T(4,128)S(1)} %get-tuple-element.24), channel_id=1, source_target_pairs={{0,5},{1,6},{2,7},{3,8},{4,9},{5,10},{6,11},{7,12},{8,13},{9,14},{... | collective-permute-start | bytes 6152 | tf_op jit(solution)/shard_map/ppermute | solution.py:25
  246.7 13.7 %collective-permute-start.20 = (f32[4,128]{1,0:T(4,128)S(1)}, f32[4,128]{1,0:T(4,128)S(1)}, u32[]{:S(2)}, u32[]{:S(2)}) collective-permute-start(f32[4,128]{1,0:T(4,128)S(1)} %get-tuple-element.24), channel_id=1, source_target_pairs={{0,6},{1,7},{2,8},{3,9},{4,10},{5,11},{6,12},{7,13},{8,14},{9,15},... | collective-permute-start | bytes 6152 | tf_op jit(solution)/shard_map/ppermute | solution.py:25
  249.4 11.0 %collective-permute-start.21 = (f32[4,128]{1,0:T(4,128)S(1)}, f32[4,128]{1,0:T(4,128)S(1)}, u32[]{:S(2)}, u32[]{:S(2)}) collective-permute-start(f32[4,128]{1,0:T(4,128)S(1)} %get-tuple-element.24), channel_id=1, source_target_pairs={{0,7},{1,8},{2,9},{3,10},{4,11},{5,12},{6,13},{7,14},{8,15},{9,0},... | collective-permute-start | bytes 6152 | tf_op jit(solution)/shard_map/ppermute | solution.py:25
  250.8 10.8 %collective-permute-start.22 = (f32[4,128]{1,0:T(4,128)S(1)}, f32[4,128]{1,0:T(4,128)S(1)}, u32[]{:S(2)}, u32[]{:S(2)}) collective-permute-start(f32[4,128]{1,0:T(4,128)S(1)} %get-tuple-element.24), channel_id=1, source_target_pairs={{0,8},{1,9},{2,10},{3,11},{4,12},{5,13},{6,14},{7,15},{8,0},{9,1},... | collective-permute-start | bytes 6152 | tf_op jit(solution)/shard_map/ppermute | solution.py:25
  252.2 11.3 %collective-permute-start.23 = (f32[4,128]{1,0:T(4,128)S(1)}, f32[4,128]{1,0:T(4,128)S(1)}, u32[]{:S(2)}, u32[]{:S(2)}) collective-permute-start(f32[4,128]{1,0:T(4,128)S(1)} %get-tuple-element.24), channel_id=1, source_target_pairs={{0,9},{1,10},{2,11},{3,12},{4,13},{5,14},{6,15},{7,0},{8,1},{9,2},... | collective-permute-start | bytes 6152 | tf_op jit(solution)/shard_map/ppermute | solution.py:25
  256.6 10.2 %collective-permute-start.24 = (f32[4,128]{1,0:T(4,128)S(1)}, f32[4,128]{1,0:T(4,128)S(1)}, u32[]{:S(2)}, u32[]{:S(2)}) collective-permute-start(f32[4,128]{1,0:T(4,128)S(1)} %get-tuple-element.24), channel_id=1, source_target_pairs={{0,10},{1,11},{2,12},{3,13},{4,14},{5,15},{6,0},{7,1},{8,2},{9,3},... | collective-permute-start | bytes 6152 | tf_op jit(solution)/shard_map/ppermute | solution.py:25
  260.4 6.4 %collective-permute-start.25 = (f32[4,128]{1,0:T(4,128)S(1)}, f32[4,128]{1,0:T(4,128)S(1)}, u32[]{:S(2)}, u32[]{:S(2)}) collective-permute-start(f32[4,128]{1,0:T(4,128)S(1)} %get-tuple-element.24), channel_id=1, source_target_pairs={{0,11},{1,12},{2,13},{3,14},{4,15},{5,0},{6,1},{7,2},{8,3},{9,4},{... | collective-permute-start | bytes 6152 | tf_op jit(solution)/shard_map/ppermute | solution.py:25
  260.4 6.4 %collective-permute-start.26 = (f32[4,128]{1,0:T(4,128)S(1)}, f32[4,128]{1,0:T(4,128)S(1)}, u32[]{:S(2)}, u32[]{:S(2)}) collective-permute-start(f32[4,128]{1,0:T(4,128)S(1)} %get-tuple-element.24), channel_id=1, source_target_pairs={{0,12},{1,13},{2,14},{3,15},{4,0},{5,1},{6,2},{7,3},{8,4},{9,5},{1... | collective-permute-start | bytes 6152 | tf_op jit(solution)/shard_map/ppermute | solution.py:25
  261.7 5.2 %collective-permute-start.27 = (f32[4,128]{1,0:T(4,128)S(1)}, f32[4,128]{1,0:T(4,128)S(1)}, u32[]{:S(2)}, u32[]{:S(2)}) collective-permute-start(f32[4,128]{1,0:T(4,128)S(1)} %get-tuple-element.24), channel_id=1, source_target_pairs={{0,13},{1,14},{2,15},{3,0},{4,1},{5,2},{6,3},{7,4},{8,5},{9,6},{10... | collective-permute-start | bytes 6152 | tf_op jit(solution)/shard_map/ppermute | solution.py:25
  263.5 5.2 %collective-permute-start.28 = (f32[4,128]{1,0:T(4,128)S(1)}, f32[4,128]{1,0:T(4,128)S(1)}, u32[]{:S(2)}, u32[]{:S(2)}) collective-permute-start(f32[4,128]{1,0:T(4,128)S(1)} %get-tuple-element.24), channel_id=1, source_target_pairs={{0,14},{1,15},{2,0},{3,1},{4,2},{5,3},{6,4},{7,5},{8,6},{9,7},{10,... | collective-permute-start | bytes 6152 | tf_op jit(solution)/shard_map/ppermute | solution.py:25
  266.8 3.6 %collective-permute-start.29 = (f32[4,128]{1,0:T(4,128)S(1)}, f32[4,128]{1,0:T(4,128)S(1)}, u32[]{:S(2)}, u32[]{:S(2)}) collective-permute-start(f32[4,128]{1,0:T(4,128)S(1)} %get-tuple-element.24), channel_id=1, source_target_pairs={{0,15},{1,0},{2,1},{3,2},{4,3},{5,4},{6,5},{7,6},{8,7},{9,8},{10,9... | collective-permute-start | bytes 6152 | tf_op jit(solution)/shard_map/ppermute | solution.py:25
Sparse Core Ops, SparseCore 0:
  43.7 116.2 all-gather.1

commit v5 on v3

--- a/solution.py
+++ b/solution.py
@@ -74,19 +74,21 @@
     kernel_part = jnp.sum(kernel)
 
     qslot = jnp.where(jnp.arange(per_dev) == 0, kernel_part, 0.0)
-    stats = jnp.stack([calib, nearest, 1.0 / norm, qslot])
+    half_inv = 0.5 / norm
+    stats = jnp.stack([calib, nearest, half_inv, qslot])
     all_stats = spread_all(stats)
     calib_cols = all_stats[0]
     nearest_cols = all_stats[1]
-    inv_norm_cols = all_stats[2]
+    half_inv_cols = all_stats[2]
     qsum = jnp.sum(all_stats[3])
+    scale = total / qsum
 
-    cond_rows = jnp.exp(-calib[:, None] * shifted) * (1.0 / norm)[:, None]
+    cond_rows = jnp.exp(-calib[:, None] * shifted) * half_inv[:, None]
     cond_cols = (
-        jnp.exp(-calib_cols[None, :] * (distance - nearest_cols[None, :])) * inv_norm_cols[None, :]
+        jnp.exp(-calib_cols[None, :] * (distance - nearest_cols[None, :])) * half_inv_cols[None, :]
     )
-    affinity = jnp.where(itself, 0.0, 0.5 * (cond_rows + cond_cols))
-    coef = (affinity - total * kernel / qsum) * kernel
+    affinity = jnp.where(itself, 0.0, cond_rows + cond_cols)
+    coef = (affinity - scale * kernel) * kernel
     force = jnp.stack([jnp.sum(coef * delta_a, axis=1), jnp.sum(coef * delta_b, axis=1)])
     return (force, calib)
 

time: 335 us -> 337 us (level)
  no operation moved by 1% of the time
where the time goes in v5:
time: 337 us; the launch traced here: 332 us
  waiting for transfers between devices  122 us (36%)
  starting transfers between devices  59 us (18%)
  other arithmetic  54.4 us (16%)
  matrix products  49.5 us (15%)
  blocking collectives  27.2 us (8%)
  between operations  15.2 us (5%)
  local copies, waits for them, and re-layouts  4.24 us (1%)
    all_gather x1, waiting for transfers between devices, spread_all(): return lax.all_gather(col_stage(values), 'row', axis=1, tiled=True)  115 us
    ppermute x30, starting transfers between devices, col_stage(): parts.append(lax.ppermute(values, 'col', pairs))  58.9 us
    dot_general x1, matrix products, body(): lax.dot_general(own_coords, all_coords, (((0,), (0,)), ((), ())), precisi...  49.5 us
    all_gather x1, blocking collectives, spread_all(): return lax.all_gather(col_stage(values), 'row', axis=1, tiled=True)  27.2 us
    reduce_sum x1, other arithmetic, body(): jnp.sum(coef * delta_a, axis=1)  25.6 us
    reduce_sum x1, other arithmetic, body(): jnp.sum(jnp.where(itself, 0.0, jnp.exp(-calib[:, None] * shifted)), axis=1)  17.8 us
    ppermute x30, waiting for transfers between devices, col_stage(): parts.append(lax.ppermute(values, 'col', pairs))  7.42 us
  transfers between devices with their start and end apart: 31, of which 5 were waited for; matrix products, arithmetic and copies ran while one was open for 0% of the time, Pallas kernels for 0%

profile of v5, /device:TPU:32, one launch (start us, length us, event | category | flops | bytes accessed | tf_op | source)
XLA Modules:
  0.0 332.0 jit_solution(9638424986140060465)
XLA Ops:
  7.2 0.0 all-gather.2.cloned.1.call-start
  7.2 0.8 multiply_reduce_fusion.1
  8.0 0.8 pad_maximum_fusion
  8.8 1.9 collective-permute-start
  10.7 1.6 collective-permute-start.1
  12.3 2.8 collective-permute-start.2
  15.1 1.6 collective-permute-start.3
  16.7 1.3 collective-permute-start.4
  17.9 3.5 %collective-permute-start.5 = (f32[67,128]{1,0:T(8,128)S(1)}, f32[67,128]{1,0:T(8,128)S(1)}, u32[]{:S(2)}, u32[]{:S(2)}) collective-permute-start(f32[67,128]{1,0:T(8,128)S(1)} %get-tuple-element.18), channel_id=1, source_target_pairs={{0,6},{1,7},{2,8},{3,9},{4,10},{5,11},{6,12},{7,13},{8,14},{9,15},... | collective-permute-start | bytes 102920 | tf_op jit(solution)/shard_map/ppermute | solution.py:25
  21.4 0.0 collective-permute-done.1
  21.4 0.6 collective-permute-start.6
  22.1 2.4 collective-permute-start.7
  24.5 4.3 %collective-permute-start.8 = (f32[67,128]{1,0:T(8,128)S(1)}, f32[67,128]{1,0:T(8,128)S(1)}, u32[]{:S(2)}, u32[]{:S(2)}) collective-permute-start(f32[67,128]{1,0:T(8,128)S(1)} %get-tuple-element.18), channel_id=1, source_target_pairs={{0,9},{1,10},{2,11},{3,12},{4,13},{5,14},{6,15},{7,0},{8,1},{9,2},... | collective-permute-start | bytes 102920 | tf_op jit(solution)/shard_map/ppermute | solution.py:25
  28.8 0.0 collective-permute-done.4
  28.8 1.3 collective-permute-start.9
  30.1 0.0 collective-permute-done.5
  30.1 1.4 collective-permute-start.10
  31.6 1.2 collective-permute-start.11
  32.8 0.0 collective-permute-done.7
  32.8 1.0 collective-permute-start.12
  33.8 5.0 %collective-permute-start.13 = (f32[67,128]{1,0:T(8,128)S(1)}, f32[67,128]{1,0:T(8,128)S(1)}, u32[]{:S(2)}, u32[]{:S(2)}) collective-permute-start(f32[67,128]{1,0:T(8,128)S(1)} %get-tuple-element.18), channel_id=1, source_target_pairs={{0,14},{1,15},{2,0},{3,1},{4,2},{5,3},{6,4},{7,5},{8,6},{9,7},{10,... | collective-permute-start | bytes 102920 | tf_op jit(solution)/shard_map/ppermute | solution.py:25
  38.8 0.0 collective-permute-start.14
  38.8 0.0 collective-permute-done.12
  38.9 2.6 collective-permute-done.13
  41.5 1.3 collective-permute-done.14
  42.7 0.8 copy-done.1
  43.5 0.0 all-gather.2.cloned.1.call-update
  43.6 0.7 neg.12
  44.2 0.8 slice_bitcast_fusion.1
  45.0 115.0 %all-gather.2.cloned.1.call-done = f32[67,32768]{1,0:T(8,128)} async-done(((f32[67,2048]{1,0:T(8,128)}), f32[67,32768]{1,0:T(8,128)}) %all-gather.2.cloned.1.call-update) | async-done | bytes 8781840 | tf_op jit(solution)/shard_map/all_gather | solution.py:30
  160.0 2.5 fusion.15
  162.5 49.5 %select_reduce_fusion.1 = (f32[128]{0:T(128)S(1)}, f32[128,32768]{0,1:T(8,128)S(1)}) fusion(s32[128]{0:T(128)S(1)} %iota_add_fusion, f32[64,128]{1,0:T(8,128)} %param.3, f32[67,32768]{1,0:T(8,128)} %all-gather.2.cloned.1.call-done, f32[32768]{0:T(1024)S(1)} %bitcast.31, f32[128]{0:T(128)S(1)} %multiply_reduce_fusion.1), kind=kOutput, calls=%fused_computation.22 | convolution fusion | flops 3250585600 | bytes 25331200 | tf_op jit(solution)/shard_map/dot_general | solution.py:49
  212.1 0.0 copy-start.3
  212.1 6.6 %multiply_reduce_fusion = (f32[128]{0:T(128)S(1)}, f32[128]{0:T(128)S(1)}, f32[128]{0:T(128)S(1)}) fusion(f32[128,32768]{0,1:T(8,128)S(1)} %get-tuple-element.25, f32[128]{0:T(128)S(1)} %get-tuple-element.24, f32[128]{0:T(128)S(1)} %neg.12, s32[128]{0:T(128)S(1)} %iota_add_fusion), kind=kLoop, calls=%fused_computation.17 | loop fusion | flops 37748352 | bytes 16780288 | tf_op jit(solution)/shard_map/reduce_sum | solution.py:66
  218.7 0.0 copy-start.2
  218.7 17.8 %select_reduce_fusion = (f32[128]{0:T(128)S(1)}, f32[]{:T(128)}) fusion(f32[128,32768]{0,1:T(8,128)S(1)} %get-tuple-element.25, f32[128]{0:T(128)S(1)} %get-tuple-element.9, f32[128]{0:T(128)S(1)} %get-tuple-element.24, s32[128]{0:T(128)S(1)} %iota_add_fusion, f32[32768]{0:T(1024)S(1)} %bitcast.26, f32[128]{0:T(128)S(1)} %get-tuple-element.23, ...), kind=kLoop, calls=%fused_computation.15 | loop fusion | flops 58720128 | bytes 17042436 | tf_op jit(solution)/shard_map/reduce_sum | solution.py:69
  236.5 0.6 compare_select_fusion
  237.2 0.2 collective-permute-start.15
  237.3 4.7 %collective-permute-start.16 = (f32[4,128]{1,0:T(4,128)S(1)}, f32[4,128]{1,0:T(4,128)S(1)}, u32[]{:S(2)}, u32[]{:S(2)}) collective-permute-start(f32[4,128]{1,0:T(4,128)S(1)} %get-tuple-element.20), channel_id=1, source_target_pairs={{0,2},{1,3},{2,4},{3,5},{4,6},{5,7},{6,8},{7,9},{8,10},{9,11},{10,... | collective-permute-start | bytes 6152 | tf_op jit(solution)/shard_map/ppermute | solution.py:25
  242.0 0.0 collective-permute-start.17
  242.0 1.5 collective-permute-start.18
  243.5 2.6 collective-permute-start.19
  246.1 0.0 collective-permute-done.15
  246.1 2.7 collective-permute-start.20
  248.8 0.0 collective-permute-done.16
  248.9 1.4 collective-permute-start.21
  250.3 0.0 collective-permute-done.17
  250.3 1.4 collective-permute-start.22
  251.7 0.0 collective-permute-done.18
  251.7 4.3 %collective-permute-start.23 = (f32[4,128]{1,0:T(4,128)S(1)}, f32[4,128]{1,0:T(4,128)S(1)}, u32[]{:S(2)}, u32[]{:S(2)}) collective-permute-start(f32[4,128]{1,0:T(4,128)S(1)} %get-tuple-element.20), channel_id=1, source_target_pairs={{0,9},{1,10},{2,11},{3,12},{4,13},{5,14},{6,15},{7,0},{8,1},{9,2},... | collective-permute-start | bytes 6152 | tf_op jit(solution)/shard_map/ppermute | solution.py:25
  256.0 0.0 collective-permute-done.19
  256.0 3.8 %collective-permute-start.24 = (f32[4,128]{1,0:T(4,128)S(1)}, f32[4,128]{1,0:T(4,128)S(1)}, u32[]{:S(2)}, u32[]{:S(2)}) collective-permute-start(f32[4,128]{1,0:T(4,128)S(1)} %get-tuple-element.20), channel_id=1, source_target_pairs={{0,10},{1,11},{2,12},{3,13},{4,14},{5,15},{6,0},{7,1},{8,2},{9,3},... | collective-permute-start | bytes 6152 | tf_op jit(solution)/shard_map/ppermute | solution.py:25
  259.9 0.0 collective-permute-done.21
  259.9 1.2 collective-permute-start.26
  261.1 0.0 collective-permute-done.22
  261.1 1.9 collective-permute-start.27
  263.0 3.3 collective-permute-start.28
  266.3 0.0 collective-permute-done.25
  266.4 1.8 collective-permute-done.28
  268.2 1.7 collective-permute-done.29
  269.9 27.2 %all_gather.7 = f32[4,32768]{1,0:T(4,128)S(1)} all-gather(f32[4,2048]{1,0:T(4,128)S(1)} %constant_dynamic-update-slice_fusion.16), channel_id=1, replica_groups=mesh['row'=16,'col'=16] {'row'}, dimensions={1}, use_global_device_ids=true | all-gather | bytes 557056 | tf_op jit(solution)/shard_map/all_gather | solution.py:30
  297.1 1.0 slice_negate_fusion
  298.7 25.6 %fusion.7 = (f32[128]{0:T(128)S(1)}, f32[128]{0:T(128)S(1)}) fusion(f32[32768]{0:T(1024)S(1)} %bitcast.25, f32[128]{0:T(128)S(1)} %get-tuple-element.22, f32[32768]{0:T(1024)S(1)} %bitcast.27, f32[128]{0:T(128)S(1)} %get-tuple-element.23, f32[]{:T(128)S(6)} %div.46, f32[32768]{0:T(1024)S(1)} %bitcast.29, f32[128,32768]{0,1:T(8,128)} %copy-done, ...), kind=kLoop, calls=%fused_computation.12 | loop fusion | flops 100663040 | bytes 17436676 | tf_op jit(solution)/shard_map/reduce_sum | solution.py:92
  324.4 0.6 pad_maximum_fusion.2
  (55 shorter events, 0.3 us)
Async XLA Ops:
  7.2 152.9 %all-gather.2.cloned.1.call-start = ((), (), s32[]{:S(2)}) async-start(), calls=%async_computation | async-start | bytes 10027008 | tf_op jit(solution)/shard_map/all_gather | solution.py:30
  8.8 9.2 %collective-permute-start = (f32[67,128]{1,0:T(8,128)S(1)}, f32[67,128]{1,0:T(8,128)S(1)}, u32[]{:S(2)}, u32[]{:S(2)}) collective-permute-start(f32[67,128]{1,0:T(8,128)S(1)} %get-tuple-element.18), channel_id=1, source_target_pairs={{0,1},{1,2},{2,3},{3,4},{4,5},{5,6},{6,7},{7,8},{8,9},{9,10},{10,1... | collective-permute-start | bytes 102920 | tf_op jit(solution)/shard_map/ppermute | solution.py:25
  10.7 10.7 %collective-permute-start.1 = (f32[67,128]{1,0:T(8,128)S(1)}, f32[67,128]{1,0:T(8,128)S(1)}, u32[]{:S(2)}, u32[]{:S(2)}) collective-permute-start(f32[67,128]{1,0:T(8,128)S(1)} %get-tuple-element.18), channel_id=1, source_target_pairs={{0,2},{1,3},{2,4},{3,5},{4,6},{5,7},{6,8},{7,9},{8,10},{9,11},{10,... | collective-permute-start | bytes 102920 | tf_op jit(solution)/shard_map/ppermute | solution.py:25
  12.3 9.8 %collective-permute-start.2 = (f32[67,128]{1,0:T(8,128)S(1)}, f32[67,128]{1,0:T(8,128)S(1)}, u32[]{:S(2)}, u32[]{:S(2)}) collective-permute-start(f32[67,128]{1,0:T(8,128)S(1)} %get-tuple-element.18), channel_id=1, source_target_pairs={{0,3},{1,4},{2,5},{3,6},{4,7},{5,8},{6,9},{7,10},{8,11},{9,12},{10... | collective-permute-start | bytes 102920 | tf_op jit(solution)/shard_map/ppermute | solution.py:25
  15.1 9.4 %collective-permute-start.3 = (f32[67,128]{1,0:T(8,128)S(1)}, f32[67,128]{1,0:T(8,128)S(1)}, u32[]{:S(2)}, u32[]{:S(2)}) collective-permute-start(f32[67,128]{1,0:T(8,128)S(1)} %get-tuple-element.18), channel_id=1, source_target_pairs={{0,4},{1,5},{2,6},{3,7},{4,8},{5,9},{6,10},{7,11},{8,12},{9,13},{1... | collective-permute-start | bytes 102920 | tf_op jit(solution)/shard_map/ppermute | solution.py:25
  16.7 12.1 %collective-permute-start.4 = (f32[67,128]{1,0:T(8,128)S(1)}, f32[67,128]{1,0:T(8,128)S(1)}, u32[]{:S(2)}, u32[]{:S(2)}) collective-permute-start(f32[67,128]{1,0:T(8,128)S(1)} %get-tuple-element.18), channel_id=1, source_target_pairs={{0,5},{1,6},{2,7},{3,8},{4,9},{5,10},{6,11},{7,12},{8,13},{9,14},{... | collective-permute-start | bytes 102920 | tf_op jit(solution)/shard_map/ppermute | solution.py:25
  17.9 12.2 %collective-permute-start.5 = (f32[67,128]{1,0:T(8,128)S(1)}, f32[67,128]{1,0:T(8,128)S(1)}, u32[]{:S(2)}, u32[]{:S(2)}) collective-permute-start(f32[67,128]{1,0:T(8,128)S(1)} %get-tuple-element.18), channel_id=1, source_target_pairs={{0,6},{1,7},{2,8},{3,9},{4,10},{5,11},{6,12},{7,13},{8,14},{9,15},... | collective-permute-start | bytes 102920 | tf_op jit(solution)/shard_map/ppermute | solution.py:25
  21.4 10.1 %collective-permute-start.6 = (f32[67,128]{1,0:T(8,128)S(1)}, f32[67,128]{1,0:T(8,128)S(1)}, u32[]{:S(2)}, u32[]{:S(2)}) collective-permute-start(f32[67,128]{1,0:T(8,128)S(1)} %get-tuple-element.18), channel_id=1, source_target_pairs={{0,7},{1,8},{2,9},{3,10},{4,11},{5,12},{6,13},{7,14},{8,15},{9,0},... | collective-permute-start | bytes 102920 | tf_op jit(solution)/shard_map/ppermute | solution.py:25
  22.1 10.7 %collective-permute-start.7 = (f32[67,128]{1,0:T(8,128)S(1)}, f32[67,128]{1,0:T(8,128)S(1)}, u32[]{:S(2)}, u32[]{:S(2)}) collective-permute-start(f32[67,128]{1,0:T(8,128)S(1)} %get-tuple-element.18), channel_id=1, source_target_pairs={{0,8},{1,9},{2,10},{3,11},{4,12},{5,13},{6,14},{7,15},{8,0},{9,1},... | collective-permute-start | bytes 102920 | tf_op jit(solution)/shard_map/ppermute | solution.py:25
  24.5 9.3 %collective-permute-start.8 = (f32[67,128]{1,0:T(8,128)S(1)}, f32[67,128]{1,0:T(8,128)S(1)}, u32[]{:S(2)}, u32[]{:S(2)}) collective-permute-start(f32[67,128]{1,0:T(8,128)S(1)} %get-tuple-element.18), channel_id=1, source_target_pairs={{0,9},{1,10},{2,11},{3,12},{4,13},{5,14},{6,15},{7,0},{8,1},{9,2},... | collective-permute-start | bytes 102920 | tf_op jit(solution)/shard_map/ppermute | solution.py:25
  28.8 10.0 %collective-permute-start.9 = (f32[67,128]{1,0:T(8,128)S(1)}, f32[67,128]{1,0:T(8,128)S(1)}, u32[]{:S(2)}, u32[]{:S(2)}) collective-permute-start(f32[67,128]{1,0:T(8,128)S(1)} %get-tuple-element.18), channel_id=1, source_target_pairs={{0,10},{1,11},{2,12},{3,13},{4,14},{5,15},{6,0},{7,1},{8,2},{9,3},... | collective-permute-start | bytes 102920 | tf_op jit(solution)/shard_map/ppermute | solution.py:25
  30.1 8.7 %collective-permute-start.10 = (f32[67,128]{1,0:T(8,128)S(1)}, f32[67,128]{1,0:T(8,128)S(1)}, u32[]{:S(2)}, u32[]{:S(2)}) collective-permute-start(f32[67,128]{1,0:T(8,128)S(1)} %get-tuple-element.18), channel_id=1, source_target_pairs={{0,11},{1,12},{2,13},{3,14},{4,15},{5,0},{6,1},{7,2},{8,3},{9,4},{... | collective-permute-start | bytes 102920 | tf_op jit(solution)/shard_map/ppermute | solution.py:25
  31.6 7.3 %collective-permute-start.11 = (f32[67,128]{1,0:T(8,128)S(1)}, f32[67,128]{1,0:T(8,128)S(1)}, u32[]{:S(2)}, u32[]{:S(2)}) collective-permute-start(f32[67,128]{1,0:T(8,128)S(1)} %get-tuple-element.18), channel_id=1, source_target_pairs={{0,12},{1,13},{2,14},{3,15},{4,0},{5,1},{6,2},{7,3},{8,4},{9,5},{1... | collective-permute-start | bytes 102920 | tf_op jit(solution)/shard_map/ppermute | solution.py:25
  32.8 6.1 %collective-permute-start.12 = (f32[67,128]{1,0:T(8,128)S(1)}, f32[67,128]{1,0:T(8,128)S(1)}, u32[]{:S(2)}, u32[]{:S(2)}) collective-permute-start(f32[67,128]{1,0:T(8,128)S(1)} %get-tuple-element.18), channel_id=1, source_target_pairs={{0,13},{1,14},{2,15},{3,0},{4,1},{5,2},{6,3},{7,4},{8,5},{9,6},{10... | collective-permute-start | bytes 102920 | tf_op jit(solution)/shard_map/ppermute | solution.py:25
  33.8 7.7 %collective-permute-start.13 = (f32[67,128]{1,0:T(8,128)S(1)}, f32[67,128]{1,0:T(8,128)S(1)}, u32[]{:S(2)}, u32[]{:S(2)}) collective-permute-start(f32[67,128]{1,0:T(8,128)S(1)} %get-tuple-element.18), channel_id=1, source_target_pairs={{0,14},{1,15},{2,0},{3,1},{4,2},{5,3},{6,4},{7,5},{8,6},{9,7},{10,... | collective-permute-start | bytes 102920 | tf_op jit(solution)/shard_map/ppermute | solution.py:25
  38.8 4.0 %collective-permute-start.14 = (f32[67,128]{1,0:T(8,128)S(1)}, f32[67,128]{1,0:T(8,128)S(1)}, u32[]{:S(2)}, u32[]{:S(2)}) collective-permute-start(f32[67,128]{1,0:T(8,128)S(1)} %get-tuple-element.18), channel_id=1, source_target_pairs={{0,15},{1,0},{2,1},{3,2},{4,3},{5,4},{6,5},{7,6},{8,7},{9,8},{10,9... | collective-permute-start | bytes 102920 | tf_op jit(solution)/shard_map/ppermute | solution.py:25
  42.7 0.8 copy-start.1
  212.1 24.4 %copy-start = (f32[128,32768]{0,1:T(8,128)}, f32[128,32768]{0,1:T(8,128)S(1)}, u32[]{:S(2)}) copy-start(f32[128,32768]{0,1:T(8,128)S(1)} %get-tuple-element.25) | copy-start | bytes 50331652
  212.1 6.6 %copy-start.3 = (f32[128]{0:T(128)S(1)}, f32[128]{0:T(128)}, u32[]{:S(2)}) copy-start(f32[128]{0:T(128)} %param.5) | copy-start | bytes 1540
  218.7 105.7 %copy-start.2 = (f32[128]{0:T(128)}, f32[128]{0:T(128)S(1)}, u32[]{:S(2)}) copy-start(f32[128]{0:T(128)S(1)} %get-tuple-element.10) | copy-start | bytes 1540
  237.2 9.0 %collective-permute-start.15 = (f32[4,128]{1,0:T(4,128)S(1)}, f32[4,128]{1,0:T(4,128)S(1)}, u32[]{:S(2)}, u32[]{:S(2)}) collective-permute-start(f32[4,128]{1,0:T(4,128)S(1)} %get-tuple-element.20), channel_id=1, source_target_pairs={{0,1},{1,2},{2,3},{3,4},{4,5},{5,6},{6,7},{7,8},{8,9},{9,10},{10,1... | collective-permute-start | bytes 6152 | tf_op jit(solution)/shard_map/ppermute | solution.py:25
  237.3 11.5 %collective-permute-start.16 = (f32[4,128]{1,0:T(4,128)S(1)}, f32[4,128]{1,0:T(4,128)S(1)}, u32[]{:S(2)}, u32[]{:S(2)}) collective-permute-start(f32[4,128]{1,0:T(4,128)S(1)} %get-tuple-element.20), channel_id=1, source_target_pairs={{0,2},{1,3},{2,4},{3,5},{4,6},{5,7},{6,8},{7,9},{8,10},{9,11},{10,... | collective-permute-start | bytes 6152 | tf_op jit(solution)/shard_map/ppermute | solution.py:25
  242.0 8.3 %collective-permute-start.17 = (f32[4,128]{1,0:T(4,128)S(1)}, f32[4,128]{1,0:T(4,128)S(1)}, u32[]{:S(2)}, u32[]{:S(2)}) collective-permute-start(f32[4,128]{1,0:T(4,128)S(1)} %get-tuple-element.20), channel_id=1, source_target_pairs={{0,3},{1,4},{2,5},{3,6},{4,7},{5,8},{6,9},{7,10},{8,11},{9,12},{10... | collective-permute-start | bytes 6152 | tf_op jit(solution)/shard_map/ppermute | solution.py:25
  242.0 9.7 %collective-permute-start.18 = (f32[4,128]{1,0:T(4,128)S(1)}, f32[4,128]{1,0:T(4,128)S(1)}, u32[]{:S(2)}, u32[]{:S(2)}) collective-permute-start(f32[4,128]{1,0:T(4,128)S(1)} %get-tuple-element.20), channel_id=1, source_target_pairs={{0,4},{1,5},{2,6},{3,7},{4,8},{5,9},{6,10},{7,11},{8,12},{9,13},{1... | collective-permute-start | bytes 6152 | tf_op jit(solution)/shard_map/ppermute | solution.py:25
  243.5 12.5 %collective-permute-start.19 = (f32[4,128]{1,0:T(4,128)S(1)}, f32[4,128]{1,0:T(4,128)S(1)}, u32[]{:S(2)}, u32[]{:S(2)}) collective-permute-start(f32[4,128]{1,0:T(4,128)S(1)} %get-tuple-element.20), channel_id=1, source_target_pairs={{0,5},{1,6},{2,7},{3,8},{4,9},{5,10},{6,11},{7,12},{8,13},{9,14},{... | collective-permute-start | bytes 6152 | tf_op jit(solution)/shard_map/ppermute | solution.py:25
  246.1 13.7 %collective-permute-start.20 = (f32[4,128]{1,0:T(4,128)S(1)}, f32[4,128]{1,0:T(4,128)S(1)}, u32[]{:S(2)}, u32[]{:S(2)}) collective-permute-start(f32[4,128]{1,0:T(4,128)S(1)} %get-tuple-element.20), channel_id=1, source_target_pairs={{0,6},{1,7},{2,8},{3,9},{4,10},{5,11},{6,12},{7,13},{8,14},{9,15},... | collective-permute-start | bytes 6152 | tf_op jit(solution)/shard_map/ppermute | solution.py:25
  248.9 11.0 %collective-permute-start.21 = (f32[4,128]{1,0:T(4,128)S(1)}, f32[4,128]{1,0:T(4,128)S(1)}, u32[]{:S(2)}, u32[]{:S(2)}) collective-permute-start(f32[4,128]{1,0:T(4,128)S(1)} %get-tuple-element.20), channel_id=1, source_target_pairs={{0,7},{1,8},{2,9},{3,10},{4,11},{5,12},{6,13},{7,14},{8,15},{9,0},... | collective-permute-start | bytes 6152 | tf_op jit(solution)/shard_map/ppermute | solution.py:25
  250.3 10.8 %collective-permute-start.22 = (f32[4,128]{1,0:T(4,128)S(1)}, f32[4,128]{1,0:T(4,128)S(1)}, u32[]{:S(2)}, u32[]{:S(2)}) collective-permute-start(f32[4,128]{1,0:T(4,128)S(1)} %get-tuple-element.20), channel_id=1, source_target_pairs={{0,8},{1,9},{2,10},{3,11},{4,12},{5,13},{6,14},{7,15},{8,0},{9,1},... | collective-permute-start | bytes 6152 | tf_op jit(solution)/shard_map/ppermute | solution.py:25
  251.7 11.3 %collective-permute-start.23 = (f32[4,128]{1,0:T(4,128)S(1)}, f32[4,128]{1,0:T(4,128)S(1)}, u32[]{:S(2)}, u32[]{:S(2)}) collective-permute-start(f32[4,128]{1,0:T(4,128)S(1)} %get-tuple-element.20), channel_id=1, source_target_pairs={{0,9},{1,10},{2,11},{3,12},{4,13},{5,14},{6,15},{7,0},{8,1},{9,2},... | collective-permute-start | bytes 6152 | tf_op jit(solution)/shard_map/ppermute | solution.py:25
  256.0 10.2 %collective-permute-start.24 = (f32[4,128]{1,0:T(4,128)S(1)}, f32[4,128]{1,0:T(4,128)S(1)}, u32[]{:S(2)}, u32[]{:S(2)}) collective-permute-start(f32[4,128]{1,0:T(4,128)S(1)} %get-tuple-element.20), channel_id=1, source_target_pairs={{0,10},{1,11},{2,12},{3,13},{4,14},{5,15},{6,0},{7,1},{8,2},{9,3},... | collective-permute-start | bytes 6152 | tf_op jit(solution)/shard_map/ppermute | solution.py:25
  259.8 6.4 %collective-permute-start.25 = (f32[4,128]{1,0:T(4,128)S(1)}, f32[4,128]{1,0:T(4,128)S(1)}, u32[]{:S(2)}, u32[]{:S(2)}) collective-permute-start(f32[4,128]{1,0:T(4,128)S(1)} %get-tuple-element.20), channel_id=1, source_target_pairs={{0,11},{1,12},{2,13},{3,14},{4,15},{5,0},{6,1},{7,2},{8,3},{9,4},{... | collective-permute-start | bytes 6152 | tf_op jit(solution)/shard_map/ppermute | solution.py:25
  259.9 6.4 %collective-permute-start.26 = (f32[4,128]{1,0:T(4,128)S(1)}, f32[4,128]{1,0:T(4,128)S(1)}, u32[]{:S(2)}, u32[]{:S(2)}) collective-permute-start(f32[4,128]{1,0:T(4,128)S(1)} %get-tuple-element.20), channel_id=1, source_target_pairs={{0,12},{1,13},{2,14},{3,15},{4,0},{5,1},{6,2},{7,3},{8,4},{9,5},{1... | collective-permute-start | bytes 6152 | tf_op jit(solution)/shard_map/ppermute | solution.py:25
  261.1 5.2 %collective-permute-start.27 = (f32[4,128]{1,0:T(4,128)S(1)}, f32[4,128]{1,0:T(4,128)S(1)}, u32[]{:S(2)}, u32[]{:S(2)}) collective-permute-start(f32[4,128]{1,0:T(4,128)S(1)} %get-tuple-element.20), channel_id=1, source_target_pairs={{0,13},{1,14},{2,15},{3,0},{4,1},{5,2},{6,3},{7,4},{8,5},{9,6},{10... | collective-permute-start | bytes 6152 | tf_op jit(solution)/shard_map/ppermute | solution.py:25
  263.0 5.2 %collective-permute-start.28 = (f32[4,128]{1,0:T(4,128)S(1)}, f32[4,128]{1,0:T(4,128)S(1)}, u32[]{:S(2)}, u32[]{:S(2)}) collective-permute-start(f32[4,128]{1,0:T(4,128)S(1)} %get-tuple-element.20), channel_id=1, source_target_pairs={{0,14},{1,15},{2,0},{3,1},{4,2},{5,3},{6,4},{7,5},{8,6},{9,7},{10,... | collective-permute-start | bytes 6152 | tf_op jit(solution)/shard_map/ppermute | solution.py:25
  266.3 3.6 %collective-permute-start.29 = (f32[4,128]{1,0:T(4,128)S(1)}, f32[4,128]{1,0:T(4,128)S(1)}, u32[]{:S(2)}, u32[]{:S(2)}) collective-permute-start(f32[4,128]{1,0:T(4,128)S(1)} %get-tuple-element.20), channel_id=1, source_target_pairs={{0,15},{1,0},{2,1},{3,2},{4,3},{5,4},{6,5},{7,6},{8,7},{9,8},{10,9... | collective-permute-start | bytes 6152 | tf_op jit(solution)/shard_map/ppermute | solution.py:25
Sparse Core Ops, SparseCore 0:
  43.7 116.2 all-gather.1

commit v6 on v3

--- a/solution.py
+++ b/solution.py
@@ -19,11 +19,13 @@
 
 def col_stage(values):
     count = lax.axis_size("col")
-    parts = [values]
-    for shift in range(1, count):
+    held = values
+    shift = 1
+    while shift < count:
         pairs = [(i, (i + shift) % count) for i in range(count)]
-        parts.append(lax.ppermute(values, "col", pairs))
-    return jnp.concatenate(parts, axis=1)
+        held = jnp.concatenate([held, lax.ppermute(held, "col", pairs)], axis=1)
+        shift *= 2
+    return held
 
 
 def spread_all(values):

time: 335 us -> 311 us (0.928)
  starting transfers between devices: 59 us -> 9.28 us
  waiting for transfers between devices: 122 us -> 155 us
  matrix products: 49.5 us -> 40.7 us
    ppermute x30 -> x8, starting transfers between devices: 58.9 us -> 9.24 us  [col_stage(): held = jnp.concatenate([held, lax.ppermute(held, 'col', pairs)], axis=1)]
    ppermute x30 -> x8, waiting for transfers between devices: 7.42 us -> 38.1 us  [col_stage(): held = jnp.concatenate([held, lax.ppermute(held, 'col', pairs)], axis=1)]
    dot_general x1, matrix products: 49.5 us -> 40.7 us  [body(): lax.dot_general(own_coords, all_coords, (((0,), (0,)), ((), ())), precisi...]
  transfers between devices with their start and end apart: 31 -> 9, of which waited for: 5 -> 9; matrix products, arithmetic and copies ran while one was open for 0% -> 0% of each run, Pallas kernels for 0% -> 0%
where the time goes in v6:
time: 311 us; the launch traced here: 305 us
  waiting for transfers between devices  155 us (50%)
  other arithmetic  54.9 us (18%)
  matrix products  40.7 us (13%)
  blocking collectives  26.4 us (8%)
  between operations  14.2 us (5%)
  starting transfers between devices  9.28 us (3%)
  local copies, waits for them, and re-layouts  4.27 us (1%)
    all_gather x1, waiting for transfers between devices, spread_all(): return lax.all_gather(col_stage(values), 'row', axis=1, tiled=True)  117 us
    dot_general x1, matrix products, body(): lax.dot_general(own_coords, all_coords, (((0,), (0,)), ((), ())), precisi...  40.7 us
    ppermute x8, waiting for transfers between devices, col_stage(): held = jnp.concatenate([held, lax.ppermute(held, 'col', pairs)], axis=1)  38.1 us
    all_gather x1, blocking collectives, spread_all(): return lax.all_gather(col_stage(values), 'row', axis=1, tiled=True)  26.4 us
    reduce_sum x1, other arithmetic, body(): jnp.sum(coef * delta_a, axis=1)  23.7 us
    reduce_sum x1, other arithmetic, body(): jnp.sum(jnp.where(itself, 0.0, jnp.exp(-calib[:, None] * shifted)), axis=1)  17.8 us
    ppermute x8, starting transfers between devices, col_stage(): held = jnp.concatenate([held, lax.ppermute(held, 'col', pairs)], axis=1)  9.24 us
    reduce_sum x1, other arithmetic, body(): second = jnp.sum(expo * shifted * shifted, axis=1)  6.56 us
  transfers between devices with their start and end apart: 9, of which 9 were waited for; matrix products, arithmetic and copies ran while one was open for 0% of the time, Pallas kernels for 0%

profile of v6, /device:TPU:32, one launch (start us, length us, event | category | flops | bytes accessed | tf_op | source)
XLA Modules:
  0.0 304.8 jit_solution(2971438880049326950)
XLA Ops:
  7.2 0.0 all-gather.2.cloned.1.call-start
  7.2 0.8 multiply_reduce_fusion.1
  8.0 0.8 pad_maximum_fusion.3
  8.8 1.9 collective-permute-start
  10.7 2.0 collective-permute-done
  12.7 0.8 pad_maximum_fusion.2
  13.5 3.3 %collective-permute-start.1 = (f32[67,256]{1,0:T(8,128)S(1)}, f32[67,256]{1,0:T(8,128)S(1)}, u32[]{:S(2)}, u32[]{:S(2)}) collective-permute-start(f32[67,256]{1,0:T(8,128)S(1)} %pad_maximum_fusion.2), channel_id=1, source_target_pairs={{0,2},{1,3},{2,4},{3,5},{4,6},{5,7},{6,8},{7,9},{8,10},{9,11},{10,... | collective-permute-start | bytes 205832 | tf_op jit(solution)/shard_map/ppermute | solution.py:26
  16.8 4.8 %collective-permute-done.1 = f32[67,256]{1,0:T(8,128)S(1)} collective-permute-done((f32[67,256]{1,0:T(8,128)S(1)}, f32[67,256]{1,0:T(8,128)S(1)}, u32[]{:S(2)}, u32[]{:S(2)}) %collective-permute-start.1) | collective-permute-done | bytes 68640 | tf_op jit(solution)/shard_map/ppermute | solution.py:26
  21.6 0.8 pad_maximum_fusion.1
  22.4 0.1 collective-permute-start.2
  22.5 6.3 %collective-permute-done.2 = f32[67,512]{1,0:T(8,128)S(1)} collective-permute-done((f32[67,512]{1,0:T(8,128)S(1)}, f32[67,512]{1,0:T(8,128)S(1)}, u32[]{:S(2)}, u32[]{:S(2)}) %collective-permute-start.2) | collective-permute-done | bytes 137248 | tf_op jit(solution)/shard_map/ppermute | solution.py:26
  28.8 0.8 pad_maximum_fusion
  29.6 0.2 collective-permute-start.3
  29.8 8.1 %collective-permute-done.3 = f32[67,1024]{1,0:T(8,128)S(1)} collective-permute-done((f32[67,1024]{1,0:T(8,128)S(1)}, f32[67,1024]{1,0:T(8,128)S(1)}, u32[]{:S(2)}, u32[]{:S(2)}) %collective-permute-start.3) | collective-permute-done | bytes 274464 | tf_op jit(solution)/shard_map/ppermute | solution.py:26
  38.0 0.0 copy-start
  38.0 0.8 copy-done
  38.8 0.0 all-gather.2.cloned.1.call-update
  38.8 0.7 neg.12
  39.5 0.8 slice_bitcast_fusion.1
  40.2 116.9 %all-gather.2.cloned.1.call-done = f32[67,32768]{1,0:T(8,128)} async-done(((f32[67,2048]{1,0:T(8,128)}), f32[67,32768]{1,0:T(8,128)}) %all-gather.2.cloned.1.call-update) | async-done | bytes 8781840 | tf_op jit(solution)/shard_map/all_gather | solution.py:32
  157.1 2.6 fusion.15
  159.8 40.7 %select_reduce_fusion.1 = (f32[128]{0:T(128)S(1)}, f32[128,32768]{0,1:T(8,128)S(1)}) fusion(s32[128]{0:T(128)S(1)} %iota_add_fusion, f32[64,128]{1,0:T(8,128)} %param.3, f32[67,32768]{1,0:T(8,128)} %all-gather.2.cloned.1.call-done, f32[32768]{0:T(1024)S(1)} %bitcast.31, f32[128]{0:T(128)S(1)} %multiply_reduce_fusion.1), kind=kOutput, calls=%fused_computation.22 | convolution fusion | flops 3250585600 | bytes 25331200 | tf_op jit(solution)/shard_map/dot_general | solution.py:51
  200.5 0.0 copy-start.2
  200.5 6.6 %multiply_reduce_fusion = (f32[128]{0:T(128)S(1)}, f32[128]{0:T(128)S(1)}, f32[128]{0:T(128)S(1)}) fusion(f32[128,32768]{0,1:T(8,128)S(1)} %get-tuple-element.25, f32[128]{0:T(128)S(1)} %get-tuple-element.24, f32[128]{0:T(128)S(1)} %neg.12, s32[128]{0:T(128)S(1)} %iota_add_fusion), kind=kLoop, calls=%fused_computation.17 | loop fusion | flops 37748352 | bytes 16780288 | tf_op jit(solution)/shard_map/reduce_sum | solution.py:68
  207.1 0.0 copy-done.2
  207.1 0.0 copy-start.1
  207.1 17.8 %select_reduce_fusion = (f32[128]{0:T(128)S(1)}, f32[]{:T(128)}) fusion(f32[128,32768]{0,1:T(8,128)S(1)} %get-tuple-element.25, f32[128]{0:T(128)S(1)} %get-tuple-element.9, f32[128]{0:T(128)S(1)} %get-tuple-element.24, s32[128]{0:T(128)S(1)} %iota_add_fusion, f32[32768]{0:T(1024)S(1)} %bitcast.26, f32[128]{0:T(128)S(1)} %get-tuple-element.23, ...), kind=kLoop, calls=%fused_computation.15 | loop fusion | flops 58720128 | bytes 17042436 | tf_op jit(solution)/shard_map/reduce_sum | solution.py:71
  224.9 0.6 compare_select_fusion
  225.6 0.2 collective-permute-start.4
  225.8 3.5 %collective-permute-done.4 = f32[4,128]{1,0:T(4,128)S(1)} collective-permute-done((f32[4,128]{1,0:T(4,128)S(1)}, f32[4,128]{1,0:T(4,128)S(1)}, u32[]{:S(2)}, u32[]{:S(2)}) %collective-permute-start.4) | collective-permute-done | bytes 2080 | tf_op jit(solution)/shard_map/ppermute | solution.py:26
  229.3 2.6 collective-permute-start.5
  231.9 4.1 %collective-permute-done.5 = f32[4,256]{1,0:T(4,128)S(1)} collective-permute-done((f32[4,256]{1,0:T(4,128)S(1)}, f32[4,256]{1,0:T(4,128)S(1)}, u32[]{:S(2)}, u32[]{:S(2)}) %collective-permute-start.5) | collective-permute-done | bytes 4128 | tf_op jit(solution)/shard_map/ppermute | solution.py:26
  236.0 0.4 collective-permute-start.6
  236.3 4.6 %collective-permute-done.6 = f32[4,512]{1,0:T(4,128)S(1)} collective-permute-done((f32[4,512]{1,0:T(4,128)S(1)}, f32[4,512]{1,0:T(4,128)S(1)}, u32[]{:S(2)}, u32[]{:S(2)}) %collective-permute-start.6) | collective-permute-done | bytes 8224 | tf_op jit(solution)/shard_map/ppermute | solution.py:26
  240.9 0.7 collective-permute-start.7
  241.6 4.6 %collective-permute-done.7 = f32[4,1024]{1,0:T(4,128)S(1)} collective-permute-done((f32[4,1024]{1,0:T(4,128)S(1)}, f32[4,1024]{1,0:T(4,128)S(1)}, u32[]{:S(2)}, u32[]{:S(2)}) %collective-permute-start.7) | collective-permute-done | bytes 16416 | tf_op jit(solution)/shard_map/ppermute | solution.py:26
  246.3 26.4 %all_gather.7 = f32[4,32768]{1,0:T(4,128)S(1)} all-gather(f32[4,2048]{1,0:T(4,128)S(1)} %constant_dynamic-update-slice_fusion.5), channel_id=1, replica_groups=mesh['row'=16,'col'=16] {'row'}, dimensions={1}, use_global_device_ids=true | all-gather | bytes 557056 | tf_op jit(solution)/shard_map/all_gather | solution.py:32
  272.7 1.0 slice_negate_fusion
  273.6 23.7 %fusion.7 = (f32[128]{0:T(128)S(1)}, f32[128]{0:T(128)S(1)}) fusion(f32[32768]{0:T(1024)S(1)} %bitcast.25, f32[128]{0:T(128)S(1)} %get-tuple-element.22, f32[32768]{0:T(1024)S(1)} %bitcast.27, f32[128]{0:T(128)S(1)} %get-tuple-element.23, f32[]{:T(128)} %get-tuple-element.15, f32[32768]{0:T(1024)S(1)} %bitcast.29, f32[128,32768]{0,1:T(8,128)S(1)} %get-tuple-element.25, ...), kind=kLoop, calls=%fused_computation.12 | loop fusion | flops 109051648 | bytes 17436676 | tf_op jit(solution)/shard_map/reduce_sum | solution.py:92
  297.4 0.0 copy-done.1
  297.4 0.6 pad_maximum_fusion.8
  (16 shorter events, 0.1 us)
Async XLA Ops:
  7.2 150.0 %all-gather.2.cloned.1.call-start = ((), (), s32[]{:S(2)}) async-start(), calls=%async_computation | async-start | bytes 10027008 | tf_op jit(solution)/shard_map/all_gather | solution.py:32
  8.8 4.0 %collective-permute-start = (f32[67,128]{1,0:T(8,128)S(1)}, f32[67,128]{1,0:T(8,128)S(1)}, u32[]{:S(2)}, u32[]{:S(2)}) collective-permute-start(f32[67,128]{1,0:T(8,128)S(1)} %get-tuple-element.18), channel_id=1, source_target_pairs={{0,1},{1,2},{2,3},{3,4},{4,5},{5,6},{6,7},{7,8},{8,9},{9,10},{10,1... | collective-permute-start | bytes 102920 | tf_op jit(solution)/shard_map/ppermute | solution.py:26
  13.5 8.1 %collective-permute-start.1 = (f32[67,256]{1,0:T(8,128)S(1)}, f32[67,256]{1,0:T(8,128)S(1)}, u32[]{:S(2)}, u32[]{:S(2)}) collective-permute-start(f32[67,256]{1,0:T(8,128)S(1)} %pad_maximum_fusion.2), channel_id=1, source_target_pairs={{0,2},{1,3},{2,4},{3,5},{4,6},{5,7},{6,8},{7,9},{8,10},{9,11},{10,... | collective-permute-start | bytes 205832 | tf_op jit(solution)/shard_map/ppermute | solution.py:26
  22.4 6.4 %collective-permute-start.2 = (f32[67,512]{1,0:T(8,128)S(1)}, f32[67,512]{1,0:T(8,128)S(1)}, u32[]{:S(2)}, u32[]{:S(2)}) collective-permute-start(f32[67,512]{1,0:T(8,128)S(1)} %pad_maximum_fusion.1), channel_id=1, source_target_pairs={{0,4},{1,5},{2,6},{3,7},{4,8},{5,9},{6,10},{7,11},{8,12},{9,13},{1... | collective-permute-start | bytes 411656 | tf_op jit(solution)/shard_map/ppermute | solution.py:26
  29.6 8.3 %collective-permute-start.3 = (f32[67,1024]{1,0:T(8,128)S(1)}, f32[67,1024]{1,0:T(8,128)S(1)}, u32[]{:S(2)}, u32[]{:S(2)}) collective-permute-start(f32[67,1024]{1,0:T(8,128)S(1)} %pad_maximum_fusion), channel_id=1, source_target_pairs={{0,8},{1,9},{2,10},{3,11},{4,12},{5,13},{6,14},{7,15},{8,0},{9,1},... | collective-permute-start | bytes 823304 | tf_op jit(solution)/shard_map/ppermute | solution.py:26
  38.0 0.8 copy-start
  200.5 6.6 %copy-start.2 = (f32[128]{0:T(128)S(1)}, f32[128]{0:T(128)}, u32[]{:S(2)}) copy-start(f32[128]{0:T(128)} %param.5) | copy-start | bytes 1540
  207.1 90.2 %copy-start.1 = (f32[128]{0:T(128)}, f32[128]{0:T(128)S(1)}, u32[]{:S(2)}) copy-start(f32[128]{0:T(128)S(1)} %get-tuple-element.10) | copy-start | bytes 1540
  225.6 3.7 %collective-permute-start.4 = (f32[4,128]{1,0:T(4,128)S(1)}, f32[4,128]{1,0:T(4,128)S(1)}, u32[]{:S(2)}, u32[]{:S(2)}) collective-permute-start(f32[4,128]{1,0:T(4,128)S(1)} %get-tuple-element.20), channel_id=1, source_target_pairs={{0,1},{1,2},{2,3},{3,4},{4,5},{5,6},{6,7},{7,8},{8,9},{9,10},{10,1... | collective-permute-start | bytes 6152 | tf_op jit(solution)/shard_map/ppermute | solution.py:26
  229.3 6.7 %collective-permute-start.5 = (f32[4,256]{1,0:T(4,128)S(1)}, f32[4,256]{1,0:T(4,128)S(1)}, u32[]{:S(2)}, u32[]{:S(2)}) collective-permute-start(f32[4,256]{1,0:T(4,128)S(1)} %pad_maximum_fusion.6), channel_id=1, source_target_pairs={{0,2},{1,3},{2,4},{3,5},{4,6},{5,7},{6,8},{7,9},{8,10},{9,11},{10,... | collective-permute-start | bytes 12296 | tf_op jit(solution)/shard_map/ppermute | solution.py:26
  236.0 4.9 %collective-permute-start.6 = (f32[4,512]{1,0:T(4,128)S(1)}, f32[4,512]{1,0:T(4,128)S(1)}, u32[]{:S(2)}, u32[]{:S(2)}) collective-permute-start(f32[4,512]{1,0:T(4,128)S(1)} %pad_maximum_fusion.5), channel_id=1, source_target_pairs={{0,4},{1,5},{2,6},{3,7},{4,8},{5,9},{6,10},{7,11},{8,12},{9,13},{1... | collective-permute-start | bytes 24584 | tf_op jit(solution)/shard_map/ppermute | solution.py:26
  240.9 5.3 %collective-permute-start.7 = (f32[4,1024]{1,0:T(4,128)S(1)}, f32[4,1024]{1,0:T(4,128)S(1)}, u32[]{:S(2)}, u32[]{:S(2)}) collective-permute-start(f32[4,1024]{1,0:T(4,128)S(1)} %pad_maximum_fusion.4), channel_id=1, source_target_pairs={{0,8},{1,9},{2,10},{3,11},{4,12},{5,13},{6,14},{7,15},{8,0},{9,1},... | collective-permute-start | bytes 49160 | tf_op jit(solution)/shard_map/ppermute | solution.py:26
Sparse Core Ops, SparseCore 0:
  38.9 118.1 all-gather.1

commit v7 on v6

--- a/solution.py
+++ b/solution.py
@@ -77,7 +77,15 @@
 
     qslot = jnp.where(jnp.arange(per_dev) == 0, kernel_part, 0.0)
     stats = jnp.stack([calib, nearest, 1.0 / norm, qslot])
-    all_stats = spread_all(stats)
+    held = col_stage(stats)
+    rows = lax.axis_size("row")
+    shift = 1
+    while shift < rows:
+        pairs = [(i, (i + shift) % rows) for i in range(rows)]
+        held = jnp.concatenate([held, lax.ppermute(held, "row", pairs)], axis=1)
+        shift *= 2
+    blocks = held.reshape(held.shape[0], rows, -1)[:, ::-1]
+    all_stats = jnp.roll(blocks, lax.axis_index("row") + 1, axis=1).reshape(held.shape)
     calib_cols = all_stats[0]
     nearest_cols = all_stats[1]
     inv_norm_cols = all_stats[2]

time: 311 us -> 335 us (1.077)
  the two profiles are of different devices: /device:TPU:32 before, /device:TPU:8 now
where the time goes in v7:
time: 335 us
  waiting for transfers between devices  207 us (62%)
  other arithmetic  57.3 us (17%)
  matrix products  41.1 us (12%)
  between operations  14.3 us (4%)
  starting transfers between devices  10.4 us (3%)
  local copies, waits for them, and re-layouts  5.05 us (2%)
    all_gather x1, waiting for transfers between devices, spread_all(): return lax.all_gather(col_stage(values), 'row', axis=1, tiled=True)  116 us
    ppermute x4, waiting for transfers between devices, body(): held = jnp.concatenate([held, lax.ppermute(held, 'row', pairs)], axis=1)  49.8 us
    dot_general x1, matrix products, body(): lax.dot_general(own_coords, all_coords, (((0,), (0,)), ((), ())), precisi...  41.1 us
    ppermute x8, waiting for transfers between devices, col_stage(): held = jnp.concatenate([held, lax.ppermute(held, 'col', pairs)], axis=1)  40.7 us
    reduce_sum x1, other arithmetic, body(): jnp.sum(coef * delta_a, axis=1)  26.3 us
    reduce_sum x1, other arithmetic, body(): jnp.sum(jnp.where(itself, 0.0, jnp.exp(-calib[:, None] * shifted)), axis=1)  17.7 us
    ppermute x8, starting transfers between devices, col_stage(): held = jnp.concatenate([held, lax.ppermute(held, 'col', pairs)], axis=1)  10 us
  transfers between devices with their start and end apart: 13, of which 13 were waited for; matrix products, arithmetic and copies ran while one was open for 0% of the time, Pallas kernels for 0%

profile of v7, /device:TPU:8, one launch (start us, length us, event | category | flops | bytes accessed | tf_op | source)
XLA Modules:
  0.0 334.7 jit_solution(1416108864164821489)
XLA Ops:
  7.2 0.0 all-gather.2.cloned.1.call-start
  7.2 0.8 multiply_reduce_fusion.1
  8.0 0.8 pad_maximum_fusion.3
  8.8 1.9 collective-permute-start
  10.7 4.7 %collective-permute-done = f32[67,128]{1,0:T(8,128)S(1)} collective-permute-done((f32[67,128]{1,0:T(8,128)S(1)}, f32[67,128]{1,0:T(8,128)S(1)}, u32[]{:S(2)}, u32[]{:S(2)}) %collective-permute-start) | collective-permute-done | bytes 34336 | tf_op jit(solution)/shard_map/ppermute | solution.py:26
  15.4 0.8 pad_maximum_fusion.2
  16.2 0.6 collective-permute-start.1
  16.8 5.6 %collective-permute-done.1 = f32[67,256]{1,0:T(8,128)S(1)} collective-permute-done((f32[67,256]{1,0:T(8,128)S(1)}, f32[67,256]{1,0:T(8,128)S(1)}, u32[]{:S(2)}, u32[]{:S(2)}) %collective-permute-start.1) | collective-permute-done | bytes 68640 | tf_op jit(solution)/shard_map/ppermute | solution.py:26
  22.4 0.8 pad_maximum_fusion.1
  23.2 1.7 collective-permute-start.2
  24.8 6.1 %collective-permute-done.2 = f32[67,512]{1,0:T(8,128)S(1)} collective-permute-done((f32[67,512]{1,0:T(8,128)S(1)}, f32[67,512]{1,0:T(8,128)S(1)}, u32[]{:S(2)}, u32[]{:S(2)}) %collective-permute-start.2) | collective-permute-done | bytes 137248 | tf_op jit(solution)/shard_map/ppermute | solution.py:26
  31.0 0.8 pad_maximum_fusion
  31.8 1.7 collective-permute-start.3
  33.5 6.6 %collective-permute-done.3 = f32[67,1024]{1,0:T(8,128)S(1)} collective-permute-done((f32[67,1024]{1,0:T(8,128)S(1)}, f32[67,1024]{1,0:T(8,128)S(1)}, u32[]{:S(2)}, u32[]{:S(2)}) %collective-permute-start.3) | collective-permute-done | bytes 274464 | tf_op jit(solution)/shard_map/ppermute | solution.py:26
  40.1 0.0 copy-start.1
  40.1 0.8 copy-done.1
  40.9 0.0 all-gather.2.cloned.1.call-update
  41.0 0.7 neg.20
  41.6 0.8 slice_bitcast_fusion.3
  42.4 116.1 %all-gather.2.cloned.1.call-done = f32[67,32768]{1,0:T(8,128)} async-done(((f32[67,2048]{1,0:T(8,128)}), f32[67,32768]{1,0:T(8,128)}) %all-gather.2.cloned.1.call-update) | async-done | bytes 8781840 | tf_op jit(solution)/shard_map/all_gather | solution.py:32
  158.5 2.5 fusion.17
  160.9 41.1 %select_reduce_fusion.1 = (f32[128]{0:T(128)S(1)}, f32[128,32768]{0,1:T(8,128)S(1)}) fusion(s32[128]{0:T(128)S(1)} %iota_add_fusion, f32[64,128]{1,0:T(8,128)} %param.3, f32[67,32768]{1,0:T(8,128)} %all-gather.2.cloned.1.call-done, f32[32768]{0:T(1024)S(1)} %bitcast.43, f32[128]{0:T(128)S(1)} %multiply_reduce_fusion.1), kind=kOutput, calls=%fused_computation.22 | convolution fusion | flops 3250585600 | bytes 25331200 | tf_op jit(solution)/shard_map/dot_general | solution.py:51
  202.1 0.0 copy-start
  202.1 0.0 copy-start.3
  202.1 6.6 %multiply_reduce_fusion = (f32[128]{0:T(128)S(1)}, f32[128]{0:T(128)S(1)}, f32[128]{0:T(128)S(1)}) fusion(f32[128,32768]{0,1:T(8,128)S(1)} %get-tuple-element.58, f32[128]{0:T(128)S(1)} %get-tuple-element.57, f32[128]{0:T(128)S(1)} %neg.20, s32[128]{0:T(128)S(1)} %iota_add_fusion), kind=kLoop, calls=%fused_computation.17 | loop fusion | flops 37748352 | bytes 16780288 | tf_op jit(solution)/shard_map/reduce_sum | solution.py:68
  208.7 0.0 copy-done.3
  208.7 0.0 copy-start.2
  208.7 17.7 %select_reduce_fusion = (f32[128]{0:T(128)S(1)}, f32[]{:T(128)}) fusion(f32[128,32768]{0,1:T(8,128)S(1)} %get-tuple-element.58, f32[128]{0:T(128)S(1)} %get-tuple-element.9, f32[128]{0:T(128)S(1)} %get-tuple-element.57, s32[128]{0:T(128)S(1)} %iota_add_fusion, f32[32768]{0:T(1024)S(1)} %bitcast.37, f32[128]{0:T(128)S(1)} %get-tuple-element.56, ...), kind=kLoop, calls=%fused_computation.15 | loop fusion | flops 58720128 | bytes 17042436 | tf_op jit(solution)/shard_map/reduce_sum | solution.py:71
  226.5 0.0 copy-done
  226.5 0.6 compare_select_fusion
  227.2 0.6 collective-permute-start.4
  227.8 5.8 %collective-permute-done.4 = f32[4,128]{1,0:T(4,128)S(1)} collective-permute-done((f32[4,128]{1,0:T(4,128)S(1)}, f32[4,128]{1,0:T(4,128)S(1)}, u32[]{:S(2)}, u32[]{:S(2)}) %collective-permute-start.4) | collective-permute-done | bytes 2080 | tf_op jit(solution)/shard_map/ppermute | solution.py:26
  233.5 0.1 collective-permute-start.5
  233.6 5.4 %collective-permute-done.5 = f32[4,256]{1,0:T(4,128)S(1)} collective-permute-done((f32[4,256]{1,0:T(4,128)S(1)}, f32[4,256]{1,0:T(4,128)S(1)}, u32[]{:S(2)}, u32[]{:S(2)}) %collective-permute-start.5) | collective-permute-done | bytes 4128 | tf_op jit(solution)/shard_map/ppermute | solution.py:26
  239.0 1.6 collective-permute-start.6
  240.6 3.1 collective-permute-done.6
  243.7 1.9 collective-permute-start.7
  245.6 3.4 %collective-permute-done.7 = f32[4,1024]{1,0:T(4,128)S(1)} collective-permute-done((f32[4,1024]{1,0:T(4,128)S(1)}, f32[4,1024]{1,0:T(4,128)S(1)}, u32[]{:S(2)}, u32[]{:S(2)}) %collective-permute-start.7) | collective-permute-done | bytes 16416 | tf_op jit(solution)/shard_map/ppermute | solution.py:26
  249.1 0.1 collective-permute-start.8
  249.2 10.9 %collective-permute-done.8 = f32[4,2048]{1,0:T(4,128)S(1)} collective-permute-done((f32[4,2048]{1,0:T(4,128)S(1)}, f32[4,2048]{1,0:T(4,128)S(1)}, u32[]{:S(2)}, u32[]{:S(2)}) %collective-permute-start.8) | collective-permute-done | bytes 32800 | tf_op jit(solution)/shard_map/ppermute | solution.py:85
  260.0 0.1 collective-permute-start.9
  260.1 14.5 %collective-permute-done.9 = f32[4,4096]{1,0:T(4,128)S(1)} collective-permute-done((f32[4,4096]{1,0:T(4,128)S(1)}, f32[4,4096]{1,0:T(4,128)S(1)}, u32[]{:S(2)}, u32[]{:S(2)}) %collective-permute-start.9) | collective-permute-done | bytes 65568 | tf_op jit(solution)/shard_map/ppermute | solution.py:85
  274.7 0.1 collective-permute-start.10
  274.8 14.1 %collective-permute-done.10 = f32[4,8192]{1,0:T(4,128)S(1)} collective-permute-done((f32[4,8192]{1,0:T(4,128)S(1)}, f32[4,8192]{1,0:T(4,128)S(1)}, u32[]{:S(2)}, u32[]{:S(2)}) %collective-permute-start.10) | collective-permute-done | bytes 131104 | tf_op jit(solution)/shard_map/ppermute | solution.py:85
  288.9 0.1 constant_dynamic-update-slice_fusion.23
  289.0 0.1 collective-permute-start.11
  289.1 10.2 %collective-permute-done.11 = f32[4,16384]{1,0:T(4,128)S(1)} collective-permute-done((f32[4,16384]{1,0:T(4,128)S(1)}, f32[4,16384]{1,0:T(4,128)S(1)}, u32[]{:S(2)}, u32[]{:S(2)}) %collective-permute-start.11) | collective-permute-done | bytes 262176 | tf_op jit(solution)/shard_map/ppermute | solution.py:85
  299.4 0.3 copy.10
  299.7 0.3 rev.3
  300.1 0.1 fusion.14
  300.2 0.6 fusion.15
  301.0 26.3 %fusion.7 = (f32[128]{0:T(128)S(1)}, f32[128]{0:T(128)S(1)}) fusion(f32[32768]{0:T(1024)S(1)} %bitcast.36, f32[128]{0:T(128)S(1)} %get-tuple-element.55, f32[32768]{0:T(1024)S(1)} %bitcast.38, f32[128]{0:T(128)S(1)} %get-tuple-element.56, f32[]{:T(128)} %get-tuple-element.17, f32[32768]{0:T(1024)S(1)} %bitcast.42, f32[128,32768]{0,1:T(8,128)} %copy-done, ...), kind=kLoop, calls=%fused_computation.12 | loop fusion | flops 109051648 | bytes 17436676 | tf_op jit(solution)/shard_map/reduce_sum | solution.py:100
  327.3 0.0 copy-done.2
  327.3 0.6 pad_maximum_fusion.8
  (23 shorter events, 0.4 us)
Async XLA Ops:
  7.2 151.3 %all-gather.2.cloned.1.call-start = ((), (), s32[]{:S(2)}) async-start(), calls=%async_computation | async-start | bytes 10027008 | tf_op jit(solution)/shard_map/all_gather | solution.py:32
  8.8 6.7 %collective-permute-start = (f32[67,128]{1,0:T(8,128)S(1)}, f32[67,128]{1,0:T(8,128)S(1)}, u32[]{:S(2)}, u32[]{:S(2)}) collective-permute-start(f32[67,128]{1,0:T(8,128)S(1)} %get-tuple-element.23), channel_id=1, source_target_pairs={{0,1},{1,2},{2,3},{3,4},{4,5},{5,6},{6,7},{7,8},{8,9},{9,10},{10,1... | collective-permute-start | bytes 102920 | tf_op jit(solution)/shard_map/ppermute | solution.py:26
  16.2 6.2 %collective-permute-start.1 = (f32[67,256]{1,0:T(8,128)S(1)}, f32[67,256]{1,0:T(8,128)S(1)}, u32[]{:S(2)}, u32[]{:S(2)}) collective-permute-start(f32[67,256]{1,0:T(8,128)S(1)} %pad_maximum_fusion.2), channel_id=1, source_target_pairs={{0,2},{1,3},{2,4},{3,5},{4,6},{5,7},{6,8},{7,9},{8,10},{9,11},{10,... | collective-permute-start | bytes 205832 | tf_op jit(solution)/shard_map/ppermute | solution.py:26
  23.2 7.8 %collective-permute-start.2 = (f32[67,512]{1,0:T(8,128)S(1)}, f32[67,512]{1,0:T(8,128)S(1)}, u32[]{:S(2)}, u32[]{:S(2)}) collective-permute-start(f32[67,512]{1,0:T(8,128)S(1)} %pad_maximum_fusion.1), channel_id=1, source_target_pairs={{0,4},{1,5},{2,6},{3,7},{4,8},{5,9},{6,10},{7,11},{8,12},{9,13},{1... | collective-permute-start | bytes 411656 | tf_op jit(solution)/shard_map/ppermute | solution.py:26
  31.8 8.3 %collective-permute-start.3 = (f32[67,1024]{1,0:T(8,128)S(1)}, f32[67,1024]{1,0:T(8,128)S(1)}, u32[]{:S(2)}, u32[]{:S(2)}) collective-permute-start(f32[67,1024]{1,0:T(8,128)S(1)} %pad_maximum_fusion), channel_id=1, source_target_pairs={{0,8},{1,9},{2,10},{3,11},{4,12},{5,13},{6,14},{7,15},{8,0},{9,1},... | collective-permute-start | bytes 823304 | tf_op jit(solution)/shard_map/ppermute | solution.py:26
  40.1 0.8 copy-start.1
  202.1 24.4 %copy-start = (f32[128,32768]{0,1:T(8,128)}, f32[128,32768]{0,1:T(8,128)S(1)}, u32[]{:S(2)}) copy-start(f32[128,32768]{0,1:T(8,128)S(1)} %get-tuple-element.58) | copy-start | bytes 50331652
  202.1 6.6 %copy-start.3 = (f32[128]{0:T(128)S(1)}, f32[128]{0:T(128)}, u32[]{:S(2)}) copy-start(f32[128]{0:T(128)} %param.5) | copy-start | bytes 1540
  208.7 118.6 %copy-start.2 = (f32[128]{0:T(128)}, f32[128]{0:T(128)S(1)}, u32[]{:S(2)}) copy-start(f32[128]{0:T(128)S(1)} %get-tuple-element.10) | copy-start | bytes 1540
  227.2 6.4 %collective-permute-start.4 = (f32[4,128]{1,0:T(4,128)S(1)}, f32[4,128]{1,0:T(4,128)S(1)}, u32[]{:S(2)}, u32[]{:S(2)}) collective-permute-start(f32[4,128]{1,0:T(4,128)S(1)} %get-tuple-element.54), channel_id=1, source_target_pairs={{0,1},{1,2},{2,3},{3,4},{4,5},{5,6},{6,7},{7,8},{8,9},{9,10},{10,1... | collective-permute-start | bytes 6152 | tf_op jit(solution)/shard_map/ppermute | solution.py:26
  233.5 5.5 %collective-permute-start.5 = (f32[4,256]{1,0:T(4,128)S(1)}, f32[4,256]{1,0:T(4,128)S(1)}, u32[]{:S(2)}, u32[]{:S(2)}) collective-permute-start(f32[4,256]{1,0:T(4,128)S(1)} %pad_maximum_fusion.6), channel_id=1, source_target_pairs={{0,2},{1,3},{2,4},{3,5},{4,6},{5,7},{6,8},{7,9},{8,10},{9,11},{10,... | collective-permute-start | bytes 12296 | tf_op jit(solution)/shard_map/ppermute | solution.py:26
  239.0 4.7 %collective-permute-start.6 = (f32[4,512]{1,0:T(4,128)S(1)}, f32[4,512]{1,0:T(4,128)S(1)}, u32[]{:S(2)}, u32[]{:S(2)}) collective-permute-start(f32[4,512]{1,0:T(4,128)S(1)} %pad_maximum_fusion.5), channel_id=1, source_target_pairs={{0,4},{1,5},{2,6},{3,7},{4,8},{5,9},{6,10},{7,11},{8,12},{9,13},{1... | collective-permute-start | bytes 24584 | tf_op jit(solution)/shard_map/ppermute | solution.py:26
  243.7 5.3 %collective-permute-start.7 = (f32[4,1024]{1,0:T(4,128)S(1)}, f32[4,1024]{1,0:T(4,128)S(1)}, u32[]{:S(2)}, u32[]{:S(2)}) collective-permute-start(f32[4,1024]{1,0:T(4,128)S(1)} %pad_maximum_fusion.4), channel_id=1, source_target_pairs={{0,8},{1,9},{2,10},{3,11},{4,12},{5,13},{6,14},{7,15},{8,0},{9,1},... | collective-permute-start | bytes 49160 | tf_op jit(solution)/shard_map/ppermute | solution.py:26
  249.1 10.9 %collective-permute-start.8 = (f32[4,2048]{1,0:T(4,128)S(1)}, f32[4,2048]{1,0:T(4,128)S(1)}, u32[]{:S(2)}, u32[]{:S(2)}) collective-permute-start(f32[4,2048]{1,0:T(4,128)S(1)} %get-tuple-element.33), channel_id=1, source_target_pairs={{0,16},{16,32},{32,48},{48,64},{64,80},{80,96},{96,112},{112,128},... | collective-permute-start | bytes 98312 | tf_op jit(solution)/shard_map/ppermute | solution.py:85
  260.0 14.6 %collective-permute-start.9 = (f32[4,4096]{1,0:T(4,128)S(1)}, f32[4,4096]{1,0:T(4,128)S(1)}, u32[]{:S(2)}, u32[]{:S(2)}) collective-permute-start(f32[4,4096]{1,0:T(4,128)S(1)} %get-tuple-element.28), channel_id=1, source_target_pairs={{0,32},{16,48},{32,64},{48,80},{64,96},{80,112},{96,128},{112,144}... | collective-permute-start | bytes 196616 | tf_op jit(solution)/shard_map/ppermute | solution.py:85
  274.7 14.2 %collective-permute-start.10 = (f32[4,8192]{1,0:T(4,128)S(1)}, f32[4,8192]{1,0:T(4,128)S(1)}, u32[]{:S(2)}, u32[]{:S(2)}) collective-permute-start(f32[4,8192]{1,0:T(4,128)S(1)} %get-tuple-element.22), channel_id=1, source_target_pairs={{0,64},{16,80},{32,96},{48,112},{64,128},{80,144},{96,160},{112,17... | collective-permute-start | bytes 393224 | tf_op jit(solution)/shard_map/ppermute | solution.py:85
  289.0 10.4 %collective-permute-start.11 = (f32[4,16384]{1,0:T(4,128)S(1)}, f32[4,16384]{1,0:T(4,128)S(1)}, u32[]{:S(2)}, u32[]{:S(2)}) collective-permute-start(f32[4,16384]{1,0:T(4,128)S(1)} %get-tuple-element.18), channel_id=1, source_target_pairs={{0,128},{16,144},{32,160},{48,176},{64,192},{80,208},{96,224},{112... | collective-permute-start | bytes 786440 | tf_op jit(solution)/shard_map/ppermute | solution.py:85
Sparse Core Ops, SparseCore 0:
  41.1 117.3 all-gather.1
